TPU v7x, 256 devices: a whole 4x4x8 slice. The times are simulated.
256 devices in a mesh: tm: 32 (over z, x_lo, core), space: 8 (over x_hi, y).
Axes of the slice: x: 4 (x_hi: 2, x_lo: 2; x = x_hi * 2 + x_lo), y: 4, z: 8, core: 2. Of those that a mesh axis runs over, the one named last changes fastest.
Arguments:
- forcing: float32 [128, 32, 128, 128], P('tm', 'space'), may hold values from -6 to 6
- conductivity: float32 [32, 128, 128], P('space'), may hold values from 0.5 to 2
- guess: float32 [32, 32, 128, 128], P('tm', 'space'), may hold values from -6 to 6
Outputs:
- solution: float32 [128, 32, 128, 128], P('tm', 'space')
All inputs are finite; a program needn't handle non-finite values.
Results may differ from a plain program's by a relative error of at most 0.00002.
Values sent between devices are 32-bit elements; how exact they have to be, the bound alone decides.
No kernel may reach another device: no remote copies, remote signals or barrier semaphores. Data moves between devices by JAX's collectives and lax.ppermute only.
A program may use at most 64 MiB of HBM per device.

v0:
```python
import jax
import jax.numpy as jnp
from jax import lax
from jax.sharding import PartitionSpec as P

CF = 4


step_length = 0.1


def extended(block, sides, width):
    for axis, dim in sides:
        count = lax.axis_size(axis)
        forward = [(i, i + 1) for i in range(count - 1)]
        backward = [(target, source) for source, target in forward]
        low = lax.ppermute(
            lax.slice_in_dim(block, block.shape[dim] - width, None, axis=dim), axis, forward
        )
        high = lax.ppermute(lax.slice_in_dim(block, 0, width, axis=dim), axis, backward)
        block = jnp.concatenate([low, block, high], axis=dim)
    return block


def shifted(value, axis, steps):
    count = lax.axis_size(axis)
    pairs = [(source, (source + steps) % count) for source in range(count)]
    return lax.ppermute(value, axis, pairs)


def neighbours(field):
    middle = field[1:-1]
    total = field[:-2] + field[2:]
    total = total + jnp.roll(middle, 1, axis=1) + jnp.roll(middle, -1, axis=1)
    return total + jnp.roll(middle, 1, axis=2) + jnp.roll(middle, -1, axis=2)


def sweep_once(field, target, weight, scaled):
    return (target + weight * neighbours(field)) / scaled


def per_device(forcing, conductivity, guess):
    stacked = jnp.concatenate([conductivity[None], forcing], axis=0)
    widened = extended(stacked, (("space", 1),), 1)
    kappa_wide = widened[0]
    fine_weight = step_length * kappa_wide
    fine_scaled = 1.0 + 6.0 * fine_weight
    coarse_weight = CF * step_length * kappa_wide
    coarse_scaled = 1.0 + 6.0 * coarse_weight

    def advance(state, weight, scaled, source):
        padded = extended(state, (("space", 0),), 2)
        target = padded[1:-1]
        if source is not None:
            target = target + step_length * source
        first = sweep_once(padded, target, weight, scaled)
        return sweep_once(first, target[1:-1], weight[1:-1], scaled[1:-1])

    def fine_step(state, index):
        return advance(state, fine_weight, fine_scaled, widened[1 + index])

    def coarse_step(state):
        return advance(state, coarse_weight, coarse_scaled, None)

    def relax(anchor):
        states = [anchor]
        for index in range(1, CF):
            states.append(fine_step(states[-1], index))
        return states

    anchor = guess[0]
    states = relax(anchor)
    before = shifted(states[-1], "tm", 1)
    defect = fine_step(before, 0) - anchor
    count = lax.axis_size("tm")

    def relay(turn, carried):
        moved = shifted(carried, "tm", 1)
        return defect + coarse_step(moved)

    total = lax.fori_loop(0, count - 1, relay, defect)
    anchor = anchor + total
    return jnp.stack(relax(anchor), axis=0)


def solution(mesh):
    in_specs = (P("tm", "space", None, None), P("space", None, None), P("tm", "space", None, None))
    out_specs = P("tm", "space", None, None)
    return jax.shard_map(
        per_device, mesh=mesh, in_specs=in_specs, out_specs=out_specs, check_vma=False
    )
```

profile of v0, /device:TPU:24, one launch (start us, length us, event | category | flops | bytes accessed | tf_op | source)
XLA Modules:
  0.0 837.5 jit_solution(8272000797384258719)
XLA Ops:
  59.3 7.9 collective-permute-done.11
  67.9 8.0 collective-permute-start.12
  88.6 704.2 %while.10 = (s32[]{:T(128)}, f32[4,128,128]{2,1,0:T(8,128)S(1)}, f32[6,128,128]{2,1,0:T(8,128)S(1)}, f32[6,128,128]{2,1,0:T(8,128)S(1)}, f32[4,128,128]{2,1,0:T(8,128)S(1)}, /*index=5*/s32[]{:T(128)}) while((s32[]{:T(128)}, f32[4,128,128]{2,1,0:T(8,128)S(1)}, f32[6,128,128]{2,1,0:T(8,128)S(1)}, f32[6,128,128]{2,1,0:T(8,128)S(1)}, ...), condition=%wide.region_1.2_spmd, body=%wide.region_0.1_spmd.sunk | while | flops 2228226 | bytes 15466685 | solution.py:81
  88.7 7.9 collective-permute-done
  111.3 7.9 collective-permute-done
  134.7 8.0 collective-permute-done
  158.8 8.0 collective-permute-done
  182.8 8.0 collective-permute-done
  205.7 7.9 collective-permute-done
  228.3 7.9 collective-permute-done
  250.9 7.9 collective-permute-done
  273.5 7.9 collective-permute-done
  296.1 7.9 collective-permute-done
  318.7 7.9 collective-permute-done
  341.2 7.9 collective-permute-done
  363.8 7.9 collective-permute-done
  386.4 7.9 collective-permute-done
  431.6 7.9 collective-permute-done
  454.2 7.9 collective-permute-done
  476.7 7.9 collective-permute-done
  499.3 7.9 collective-permute-done
  521.9 7.9 collective-permute-done
  544.5 7.9 collective-permute-done
  567.1 7.9 collective-permute-done
  589.7 7.9 collective-permute-done
  634.8 7.9 collective-permute-done
  657.4 7.9 collective-permute-done
  680.0 7.9 collective-permute-done
  702.6 7.9 collective-permute-done
  725.2 7.9 collective-permute-done
  747.7 7.9 collective-permute-done
  770.3 7.9 collective-permute-done
  (727 shorter events, 588.4 us)
Async XLA Ops:
  1.0 17.1 %collective-permute-start.3 = (f32[2,128,128]{2,1,0:T(8,128)S(1)}, f32[2,128,128]{2,1,0:T(8,128)S(1)}, u32[]{:S(2)}, u32[]{:S(2)}) collective-permute-start(f32[2,128,128]{2,1,0:T(8,128)S(1)} %get-tuple-element.193), channel_id=1, source_target_pairs={{0,1},{1,2},{2,3},{3,4},{4,5},{5,6},{6,7},{8,9},{9,10},{10,11},{11... | collective-permute-start | bytes 393224 | tf_op jit(solution)/shard_map/ppermute | solution.py:17
  5.6 12.5 %collective-permute-start.4 = (f32[2,128,128]{2,1,0:T(8,128)S(1)}, f32[2,128,128]{2,1,0:T(8,128)S(1)}, u32[]{:S(2)}, u32[]{:S(2)}) collective-permute-start(f32[2,128,128]{2,1,0:T(8,128)S(1)} %get-tuple-element.194), channel_id=1, source_target_pairs={{1,0},{2,1},{3,2},{4,3},{5,4},{6,5},{7,6},{9,8},{10,9},{11,10},{12... | collective-permute-start | bytes 393224 | tf_op jit(solution)/shard_map/ppermute | solution.py:20
  8.7 13.9 %collective-permute-start.5 = (f32[5,1,128,128]{3,2,1,0:T(8,128)S(1)}, f32[5,1,128,128]{3,2,1,0:T(8,128)S(1)}, u32[]{:S(2)}, u32[]{:S(2)}) collective-permute-start(f32[5,1,128,128]{3,2,1,0:T(8,128)S(1)} %get-tuple-element.79), channel_id=1, source_target_pairs={{0,1},{1,2},{2,3},{3,4},{4,5},{5,6},{6,7},{8,9},{9,10},{10,11},{11... | collective-permute-start | bytes 983048 | tf_op jit(solution)/shard_map/ppermute | solution.py:17
  16.2 14.1 %collective-permute-start.6 = (f32[5,1,128,128]{3,2,1,0:T(8,128)S(1)}, f32[5,1,128,128]{3,2,1,0:T(8,128)S(1)}, u32[]{:S(2)}, u32[]{:S(2)}) collective-permute-start(f32[5,1,128,128]{3,2,1,0:T(8,128)S(1)} %get-tuple-element.80), channel_id=1, source_target_pairs={{1,0},{2,1},{3,2},{4,3},{5,4},{6,5},{7,6},{9,8},{10,9},{11,10},{12... | collective-permute-start | bytes 983048 | tf_op jit(solution)/shard_map/ppermute | solution.py:20
  33.6 10.5 %collective-permute-start.8 = (f32[2,128,128]{2,1,0:T(8,128)S(1)}, f32[2,128,128]{2,1,0:T(8,128)S(1)}, u32[]{:S(2)}, u32[]{:S(2)}) collective-permute-start(f32[2,128,128]{2,1,0:T(8,128)S(1)} %get-tuple-element.192), channel_id=1, source_target_pairs={{1,0},{2,1},{3,2},{4,3},{5,4},{6,5},{7,6},{9,8},{10,9},{11,10},{12... | collective-permute-start | bytes 393224 | tf_op jit(solution)/shard_map/ppermute | solution.py:20
  45.7 10.5 %collective-permute-start.10 = (f32[2,128,128]{2,1,0:T(8,128)S(1)}, f32[2,128,128]{2,1,0:T(8,128)S(1)}, u32[]{:S(2)}, u32[]{:S(2)}) collective-permute-start(f32[2,128,128]{2,1,0:T(8,128)S(1)} %get-tuple-element.190), channel_id=1, source_target_pairs={{1,0},{2,1},{3,2},{4,3},{5,4},{6,5},{7,6},{9,8},{10,9},{11,10},{12... | collective-permute-start | bytes 393224 | tf_op jit(solution)/shard_map/ppermute | solution.py:20
  67.9 10.8 %collective-permute-start.12 = (f32[2,128,128]{2,1,0:T(8,128)}, f32[2,128,128]{2,1,0:T(8,128)S(1)}, u32[]{:S(2)}, u32[]{:S(2)}) collective-permute-start(f32[2,128,128]{2,1,0:T(8,128)} %get-tuple-element.188), channel_id=1, source_target_pairs={{0,1},{1,2},{2,3},{3,4},{4,5},{5,6},{6,7},{8,9},{9,10},{10,11},{11... | collective-permute-start | bytes 393224 | tf_op jit(solution)/shard_map/ppermute | solution.py:17
  75.8 10.5 %collective-permute-start.13 = (f32[2,128,128]{2,1,0:T(8,128)S(1)}, f32[2,128,128]{2,1,0:T(8,128)S(1)}, u32[]{:S(2)}, u32[]{:S(2)}) collective-permute-start(f32[2,128,128]{2,1,0:T(8,128)S(1)} %get-tuple-element.187), channel_id=1, source_target_pairs={{1,0},{2,1},{3,2},{4,3},{5,4},{6,5},{7,6},{9,8},{10,9},{11,10},{12... | collective-permute-start | bytes 393224 | tf_op jit(solution)/shard_map/ppermute | solution.py:20
  99.2 10.5 %collective-permute-start.2 = (f32[2,128,128]{2,1,0:T(8,128)S(1)}, f32[2,128,128]{2,1,0:T(8,128)S(1)}, u32[]{:S(2)}, u32[]{:S(2)}) collective-permute-start(f32[2,128,128]{2,1,0:T(8,128)S(1)} %get-tuple-element.245), channel_id=1, source_target_pairs={{1,0},{2,1},{3,2},{4,3},{5,4},{6,5},{7,6},{9,8},{10,9},{11,10},{12... | collective-permute-start | bytes 393224 | tf_op jit(solution)/shard_map/while/body/eval_jaxpr/ppermute | solution.py:20
  121.9 11.3 %collective-permute-start.2 = (f32[2,128,128]{2,1,0:T(8,128)S(1)}, f32[2,128,128]{2,1,0:T(8,128)S(1)}, u32[]{:S(2)}, u32[]{:S(2)}) collective-permute-start(f32[2,128,128]{2,1,0:T(8,128)S(1)} %get-tuple-element.245), channel_id=1, source_target_pairs={{1,0},{2,1},{3,2},{4,3},{5,4},{6,5},{7,6},{9,8},{10,9},{11,10},{12... | collective-permute-start | bytes 393224 | tf_op jit(solution)/shard_map/while/body/eval_jaxpr/ppermute | solution.py:20
  145.3 11.9 %collective-permute-start.2 = (f32[2,128,128]{2,1,0:T(8,128)S(1)}, f32[2,128,128]{2,1,0:T(8,128)S(1)}, u32[]{:S(2)}, u32[]{:S(2)}) collective-permute-start(f32[2,128,128]{2,1,0:T(8,128)S(1)} %get-tuple-element.245), channel_id=1, source_target_pairs={{1,0},{2,1},{3,2},{4,3},{5,4},{6,5},{7,6},{9,8},{10,9},{11,10},{12... | collective-permute-start | bytes 393224 | tf_op jit(solution)/shard_map/while/body/eval_jaxpr/ppermute | solution.py:20
  169.4 11.8 %collective-permute-start.2 = (f32[2,128,128]{2,1,0:T(8,128)S(1)}, f32[2,128,128]{2,1,0:T(8,128)S(1)}, u32[]{:S(2)}, u32[]{:S(2)}) collective-permute-start(f32[2,128,128]{2,1,0:T(8,128)S(1)} %get-tuple-element.245), channel_id=1, source_target_pairs={{1,0},{2,1},{3,2},{4,3},{5,4},{6,5},{7,6},{9,8},{10,9},{11,10},{12... | collective-permute-start | bytes 393224 | tf_op jit(solution)/shard_map/while/body/eval_jaxpr/ppermute | solution.py:20
  193.4 10.7 %collective-permute-start.2 = (f32[2,128,128]{2,1,0:T(8,128)S(1)}, f32[2,128,128]{2,1,0:T(8,128)S(1)}, u32[]{:S(2)}, u32[]{:S(2)}) collective-permute-start(f32[2,128,128]{2,1,0:T(8,128)S(1)} %get-tuple-element.245), channel_id=1, source_target_pairs={{1,0},{2,1},{3,2},{4,3},{5,4},{6,5},{7,6},{9,8},{10,9},{11,10},{12... | collective-permute-start | bytes 393224 | tf_op jit(solution)/shard_map/while/body/eval_jaxpr/ppermute | solution.py:20
  216.2 10.5 %collective-permute-start.2 = (f32[2,128,128]{2,1,0:T(8,128)S(1)}, f32[2,128,128]{2,1,0:T(8,128)S(1)}, u32[]{:S(2)}, u32[]{:S(2)}) collective-permute-start(f32[2,128,128]{2,1,0:T(8,128)S(1)} %get-tuple-element.245), channel_id=1, source_target_pairs={{1,0},{2,1},{3,2},{4,3},{5,4},{6,5},{7,6},{9,8},{10,9},{11,10},{12... | collective-permute-start | bytes 393224 | tf_op jit(solution)/shard_map/while/body/eval_jaxpr/ppermute | solution.py:20
  238.8 10.5 %collective-permute-start.2 = (f32[2,128,128]{2,1,0:T(8,128)S(1)}, f32[2,128,128]{2,1,0:T(8,128)S(1)}, u32[]{:S(2)}, u32[]{:S(2)}) collective-permute-start(f32[2,128,128]{2,1,0:T(8,128)S(1)} %get-tuple-element.245), channel_id=1, source_target_pairs={{1,0},{2,1},{3,2},{4,3},{5,4},{6,5},{7,6},{9,8},{10,9},{11,10},{12... | collective-permute-start | bytes 393224 | tf_op jit(solution)/shard_map/while/body/eval_jaxpr/ppermute | solution.py:20
  261.4 10.5 %collective-permute-start.2 = (f32[2,128,128]{2,1,0:T(8,128)S(1)}, f32[2,128,128]{2,1,0:T(8,128)S(1)}, u32[]{:S(2)}, u32[]{:S(2)}) collective-permute-start(f32[2,128,128]{2,1,0:T(8,128)S(1)} %get-tuple-element.245), channel_id=1, source_target_pairs={{1,0},{2,1},{3,2},{4,3},{5,4},{6,5},{7,6},{9,8},{10,9},{11,10},{12... | collective-permute-start | bytes 393224 | tf_op jit(solution)/shard_map/while/body/eval_jaxpr/ppermute | solution.py:20
  284.0 10.5 %collective-permute-start.2 = (f32[2,128,128]{2,1,0:T(8,128)S(1)}, f32[2,128,128]{2,1,0:T(8,128)S(1)}, u32[]{:S(2)}, u32[]{:S(2)}) collective-permute-start(f32[2,128,128]{2,1,0:T(8,128)S(1)} %get-tuple-element.245), channel_id=1, source_target_pairs={{1,0},{2,1},{3,2},{4,3},{5,4},{6,5},{7,6},{9,8},{10,9},{11,10},{12... | collective-permute-start | bytes 393224 | tf_op jit(solution)/shard_map/while/body/eval_jaxpr/ppermute | solution.py:20
  306.6 10.5 %collective-permute-start.2 = (f32[2,128,128]{2,1,0:T(8,128)S(1)}, f32[2,128,128]{2,1,0:T(8,128)S(1)}, u32[]{:S(2)}, u32[]{:S(2)}) collective-permute-start(f32[2,128,128]{2,1,0:T(8,128)S(1)} %get-tuple-element.245), channel_id=1, source_target_pairs={{1,0},{2,1},{3,2},{4,3},{5,4},{6,5},{7,6},{9,8},{10,9},{11,10},{12... | collective-permute-start | bytes 393224 | tf_op jit(solution)/shard_map/while/body/eval_jaxpr/ppermute | solution.py:20
  329.2 10.5 %collective-permute-start.2 = (f32[2,128,128]{2,1,0:T(8,128)S(1)}, f32[2,128,128]{2,1,0:T(8,128)S(1)}, u32[]{:S(2)}, u32[]{:S(2)}) collective-permute-start(f32[2,128,128]{2,1,0:T(8,128)S(1)} %get-tuple-element.245), channel_id=1, source_target_pairs={{1,0},{2,1},{3,2},{4,3},{5,4},{6,5},{7,6},{9,8},{10,9},{11,10},{12... | collective-permute-start | bytes 393224 | tf_op jit(solution)/shard_map/while/body/eval_jaxpr/ppermute | solution.py:20
  351.7 10.5 %collective-permute-start.2 = (f32[2,128,128]{2,1,0:T(8,128)S(1)}, f32[2,128,128]{2,1,0:T(8,128)S(1)}, u32[]{:S(2)}, u32[]{:S(2)}) collective-permute-start(f32[2,128,128]{2,1,0:T(8,128)S(1)} %get-tuple-element.245), channel_id=1, source_target_pairs={{1,0},{2,1},{3,2},{4,3},{5,4},{6,5},{7,6},{9,8},{10,9},{11,10},{12... | collective-permute-start | bytes 393224 | tf_op jit(solution)/shard_map/while/body/eval_jaxpr/ppermute | solution.py:20
  374.3 10.5 %collective-permute-start.2 = (f32[2,128,128]{2,1,0:T(8,128)S(1)}, f32[2,128,128]{2,1,0:T(8,128)S(1)}, u32[]{:S(2)}, u32[]{:S(2)}) collective-permute-start(f32[2,128,128]{2,1,0:T(8,128)S(1)} %get-tuple-element.245), channel_id=1, source_target_pairs={{1,0},{2,1},{3,2},{4,3},{5,4},{6,5},{7,6},{9,8},{10,9},{11,10},{12... | collective-permute-start | bytes 393224 | tf_op jit(solution)/shard_map/while/body/eval_jaxpr/ppermute | solution.py:20
  396.9 10.5 %collective-permute-start.2 = (f32[2,128,128]{2,1,0:T(8,128)S(1)}, f32[2,128,128]{2,1,0:T(8,128)S(1)}, u32[]{:S(2)}, u32[]{:S(2)}) collective-permute-start(f32[2,128,128]{2,1,0:T(8,128)S(1)} %get-tuple-element.245), channel_id=1, source_target_pairs={{1,0},{2,1},{3,2},{4,3},{5,4},{6,5},{7,6},{9,8},{10,9},{11,10},{12... | collective-permute-start | bytes 393224 | tf_op jit(solution)/shard_map/while/body/eval_jaxpr/ppermute | solution.py:20
  419.5 10.5 %collective-permute-start.2 = (f32[2,128,128]{2,1,0:T(8,128)S(1)}, f32[2,128,128]{2,1,0:T(8,128)S(1)}, u32[]{:S(2)}, u32[]{:S(2)}) collective-permute-start(f32[2,128,128]{2,1,0:T(8,128)S(1)} %get-tuple-element.245), channel_id=1, source_target_pairs={{1,0},{2,1},{3,2},{4,3},{5,4},{6,5},{7,6},{9,8},{10,9},{11,10},{12... | collective-permute-start | bytes 393224 | tf_op jit(solution)/shard_map/while/body/eval_jaxpr/ppermute | solution.py:20
  442.1 10.5 %collective-permute-start.2 = (f32[2,128,128]{2,1,0:T(8,128)S(1)}, f32[2,128,128]{2,1,0:T(8,128)S(1)}, u32[]{:S(2)}, u32[]{:S(2)}) collective-permute-start(f32[2,128,128]{2,1,0:T(8,128)S(1)} %get-tuple-element.245), channel_id=1, source_target_pairs={{1,0},{2,1},{3,2},{4,3},{5,4},{6,5},{7,6},{9,8},{10,9},{11,10},{12... | collective-permute-start | bytes 393224 | tf_op jit(solution)/shard_map/while/body/eval_jaxpr/ppermute | solution.py:20
  464.7 10.5 %collective-permute-start.2 = (f32[2,128,128]{2,1,0:T(8,128)S(1)}, f32[2,128,128]{2,1,0:T(8,128)S(1)}, u32[]{:S(2)}, u32[]{:S(2)}) collective-permute-start(f32[2,128,128]{2,1,0:T(8,128)S(1)} %get-tuple-element.245), channel_id=1, source_target_pairs={{1,0},{2,1},{3,2},{4,3},{5,4},{6,5},{7,6},{9,8},{10,9},{11,10},{12... | collective-permute-start | bytes 393224 | tf_op jit(solution)/shard_map/while/body/eval_jaxpr/ppermute | solution.py:20
  487.2 10.5 %collective-permute-start.2 = (f32[2,128,128]{2,1,0:T(8,128)S(1)}, f32[2,128,128]{2,1,0:T(8,128)S(1)}, u32[]{:S(2)}, u32[]{:S(2)}) collective-permute-start(f32[2,128,128]{2,1,0:T(8,128)S(1)} %get-tuple-element.245), channel_id=1, source_target_pairs={{1,0},{2,1},{3,2},{4,3},{5,4},{6,5},{7,6},{9,8},{10,9},{11,10},{12... | collective-permute-start | bytes 393224 | tf_op jit(solution)/shard_map/while/body/eval_jaxpr/ppermute | solution.py:20
  509.8 10.5 %collective-permute-start.2 = (f32[2,128,128]{2,1,0:T(8,128)S(1)}, f32[2,128,128]{2,1,0:T(8,128)S(1)}, u32[]{:S(2)}, u32[]{:S(2)}) collective-permute-start(f32[2,128,128]{2,1,0:T(8,128)S(1)} %get-tuple-element.245), channel_id=1, source_target_pairs={{1,0},{2,1},{3,2},{4,3},{5,4},{6,5},{7,6},{9,8},{10,9},{11,10},{12... | collective-permute-start | bytes 393224 | tf_op jit(solution)/shard_map/while/body/eval_jaxpr/ppermute | solution.py:20
  532.4 10.5 %collective-permute-start.2 = (f32[2,128,128]{2,1,0:T(8,128)S(1)}, f32[2,128,128]{2,1,0:T(8,128)S(1)}, u32[]{:S(2)}, u32[]{:S(2)}) collective-permute-start(f32[2,128,128]{2,1,0:T(8,128)S(1)} %get-tuple-element.245), channel_id=1, source_target_pairs={{1,0},{2,1},{3,2},{4,3},{5,4},{6,5},{7,6},{9,8},{10,9},{11,10},{12... | collective-permute-start | bytes 393224 | tf_op jit(solution)/shard_map/while/body/eval_jaxpr/ppermute | solution.py:20
  555.0 10.5 %collective-permute-start.2 = (f32[2,128,128]{2,1,0:T(8,128)S(1)}, f32[2,128,128]{2,1,0:T(8,128)S(1)}, u32[]{:S(2)}, u32[]{:S(2)}) collective-permute-start(f32[2,128,128]{2,1,0:T(8,128)S(1)} %get-tuple-element.245), channel_id=1, source_target_pairs={{1,0},{2,1},{3,2},{4,3},{5,4},{6,5},{7,6},{9,8},{10,9},{11,10},{12... | collective-permute-start | bytes 393224 | tf_op jit(solution)/shard_map/while/body/eval_jaxpr/ppermute | solution.py:20
  577.6 10.5 %collective-permute-start.2 = (f32[2,128,128]{2,1,0:T(8,128)S(1)}, f32[2,128,128]{2,1,0:T(8,128)S(1)}, u32[]{:S(2)}, u32[]{:S(2)}) collective-permute-start(f32[2,128,128]{2,1,0:T(8,128)S(1)} %get-tuple-element.245), channel_id=1, source_target_pairs={{1,0},{2,1},{3,2},{4,3},{5,4},{6,5},{7,6},{9,8},{10,9},{11,10},{12... | collective-permute-start | bytes 393224 | tf_op jit(solution)/shard_map/while/body/eval_jaxpr/ppermute | solution.py:20
  600.1 10.5 %collective-permute-start.2 = (f32[2,128,128]{2,1,0:T(8,128)S(1)}, f32[2,128,128]{2,1,0:T(8,128)S(1)}, u32[]{:S(2)}, u32[]{:S(2)}) collective-permute-start(f32[2,128,128]{2,1,0:T(8,128)S(1)} %get-tuple-element.245), channel_id=1, source_target_pairs={{1,0},{2,1},{3,2},{4,3},{5,4},{6,5},{7,6},{9,8},{10,9},{11,10},{12... | collective-permute-start | bytes 393224 | tf_op jit(solution)/shard_map/while/body/eval_jaxpr/ppermute | solution.py:20
  622.7 10.5 %collective-permute-start.2 = (f32[2,128,128]{2,1,0:T(8,128)S(1)}, f32[2,128,128]{2,1,0:T(8,128)S(1)}, u32[]{:S(2)}, u32[]{:S(2)}) collective-permute-start(f32[2,128,128]{2,1,0:T(8,128)S(1)} %get-tuple-element.245), channel_id=1, source_target_pairs={{1,0},{2,1},{3,2},{4,3},{5,4},{6,5},{7,6},{9,8},{10,9},{11,10},{12... | collective-permute-start | bytes 393224 | tf_op jit(solution)/shard_map/while/body/eval_jaxpr/ppermute | solution.py:20
  (87 other events, 718.1 us)
where the time goes:
time: 840 us; the launch traced here: 838 us
  waiting for transfers between devices  507 us (60%)
  starting transfers between devices  242 us (29%)
  local copies, waits for them, and re-layouts  53.6 us (6%)
  other arithmetic  30.7 us (4%)
    ppermute x32, waiting for transfers between devices, shifted(): return lax.ppermute(value, axis, pairs)  253 us
    ppermute x39, waiting for transfers between devices, extended(): lax.ppermute(lax.slice_in_dim(block, 0, width, axis=dim), axis, backward)  206 us
    ppermute x39, starting transfers between devices, extended(): lax.ppermute(lax.slice_in_dim(block, 0, width, axis=dim), axis, backward)  145 us
    ppermute x39, starting transfers between devices, extended(): lax.ppermute(lax.slice_in_dim(block, block.shape[dim] - width, None, axis...  94.4 us
    ppermute x39, waiting for transfers between devices, extended(): lax.ppermute(lax.slice_in_dim(block, block.shape[dim] - width, None, axis...  47.8 us
    slice x152, local copies, waits for them, and re-layouts, neighbours(): return total + jnp.roll(middle, 1, axis=2) + jnp.roll(middle, -1, axis=2)  23.8 us
    slice x32, local copies, waits for them, and re-layouts, extended(): lax.slice_in_dim(block, 0, width, axis=dim)  21.9 us
    div x43, other arithmetic, sweep_once(): return (target + weight * neighbours(field)) / scaled  16.9 us
  transfers between devices with their start and end apart: 110, of which 108 were waited for; matrix products, arithmetic and copies ran while one was open for 0% of the time, Pallas kernels for 0%

commit v1 on v0

--- a/solution.py
+++ b/solution.py
@@ -35,6 +35,11 @@
     return total + jnp.roll(middle, 1, axis=2) + jnp.roll(middle, -1, axis=2)
 
 
+def neighbours_closed(field):
+    zero = jnp.zeros_like(field[:1])
+    return neighbours(jnp.concatenate([zero, field, zero], axis=0))
+
+
 def sweep_once(field, target, weight, scaled):
     return (target + weight * neighbours(field)) / scaled
 
@@ -45,7 +50,9 @@
     kappa_wide = widened[0]
     fine_weight = step_length * kappa_wide
     fine_scaled = 1.0 + 6.0 * fine_weight
-    coarse_weight = CF * step_length * kappa_wide
+
+    kappa_full = lax.all_gather(conductivity, "space", axis=0, tiled=True)
+    coarse_weight = CF * step_length * kappa_full
     coarse_scaled = 1.0 + 6.0 * coarse_weight
 
     def advance(state, weight, scaled, source):
@@ -59,8 +66,9 @@
     def fine_step(state, index):
         return advance(state, fine_weight, fine_scaled, widened[1 + index])
 
-    def coarse_step(state):
-        return advance(state, coarse_weight, coarse_scaled, None)
+    def coarse_full(field):
+        first = (field + coarse_weight * neighbours_closed(field)) / coarse_scaled
+        return (field + coarse_weight * neighbours_closed(first)) / coarse_scaled
 
     def relax(anchor):
         states = [anchor]
@@ -72,13 +80,25 @@
     states = relax(anchor)
     before = shifted(states[-1], "tm", 1)
     defect = fine_step(before, 0) - anchor
+
     count = lax.axis_size("tm")
+    me = lax.axis_index("tm")
+    depth = defect.shape[0]
+    offset = lax.axis_index("space") * depth
+    defect_full = lax.all_gather(defect, "space", axis=0, tiled=True)
 
-    def relay(turn, carried):
-        moved = shifted(carried, "tm", 1)
-        return defect + coarse_step(moved)
+    blocks = jnp.zeros((count,) + defect.shape, defect.dtype)
+    blocks = lax.dynamic_update_index_in_dim(blocks, defect, me, 0)
 
-    total = lax.fori_loop(0, count - 1, relay, defect)
+    def chain(power, carried):
+        field, blocks = carried
+        field = coarse_full(field)
+        piece = lax.dynamic_slice_in_dim(field, offset, depth, axis=0)
+        blocks = lax.dynamic_update_index_in_dim(blocks, piece, (me + power) % count, 0)
+        return field, blocks
+
+    _, blocks = lax.fori_loop(1, count, chain, (defect_full, blocks))
+    total = lax.psum_scatter(blocks, "tm", scatter_dimension=0, tiled=True)[0]
     anchor = anchor + total
     return jnp.stack(relax(anchor), axis=0)
 

time: 840 us -> 823 us (0.980)
  local copies, waits for them, and re-layouts: 53.6 us -> 302 us
  waiting for transfers between devices: 507 us -> 271 us
  starting transfers between devices: 242 us -> 52.2 us
  other arithmetic: 30.7 us -> 179 us
  between operations: 0.68 us -> 13.8 us
    ppermute x32 -> x1, waiting for transfers between devices: 253 us -> 7.89 us  [shifted(): return lax.ppermute(value, axis, pairs)]
    div x0 -> x62, other arithmetic: none -> 165 us  [the longest x31 86.4 us: coarse_full(): return (field + coarse_weight * neighbours_closed(first)) / coarse_scaled]
    ppermute x39 -> x8, waiting for transfers between devices: 206 us -> 42 us  [extended(): lax.ppermute(lax.slice_in_dim(block, 0, width, axis=dim), axis, backward)]
    reduce_scatter x0 -> x1, waiting for transfers between devices: none -> 131 us  [per_device(): total = lax.psum_scatter(blocks, 'tm', scatter_dimension=0, tiled=True)[0]]
    ppermute x39 -> x8, starting transfers between devices: 145 us -> 25.4 us  [extended(): lax.ppermute(lax.slice_in_dim(block, 0, width, axis=dim), axis, backward)]
    slice x146, local copies, waits for them, and re-layouts: 3.92 us -> 107 us  [neighbours(): total = total + jnp.roll(middle, 1, axis=1) + jnp.roll(middle, -1, axis=1)]
    all_gather x0 -> x2, waiting for transfers between devices: none -> 79.6 us  [the longest x1 54.9 us: per_device(): defect_full = lax.all_gather(defect, 'space', axis=0, tiled=True)]
    slice x152, local copies, waits for them, and re-layouts: 23.8 us -> 101 us  [neighbours(): return total + jnp.roll(middle, 1, axis=2) + jnp.roll(middle, -1, axis=2)]
  transfers between devices with their start and end apart: 110 -> 20, of which waited for: 108 -> 18; matrix products, arithmetic and copies ran while one was open for 0% -> 2% of each run, Pallas kernels for 0% -> 0%
where the time goes in v1:
time: 823 us; the launch traced here: 822 us
  local copies, waits for them, and re-layouts  302 us (37%)
  waiting for transfers between devices  271 us (33%)
  other arithmetic  179 us (22%)
  starting transfers between devices  52.2 us (6%)
  between operations  13.8 us (2%)
    reduce_scatter x1, waiting for transfers between devices, per_device(): total = lax.psum_scatter(blocks, 'tm', scatter_dimension=0, tiled=True)[0]  131 us
    slice x146, local copies, waits for them, and re-layouts, neighbours(): total = total + jnp.roll(middle, 1, axis=1) + jnp.roll(middle, -1, axis=1)  107 us
    slice x152, local copies, waits for them, and re-layouts, neighbours(): return total + jnp.roll(middle, 1, axis=2) + jnp.roll(middle, -1, axis=2)  101 us
    div x31, other arithmetic, coarse_full(): return (field + coarse_weight * neighbours_closed(first)) / coarse_scaled  86.4 us
    div x31, other arithmetic, coarse_full(): first = (field + coarse_weight * neighbours_closed(field)) / coarse_scaled  78.6 us
    while x248, local copies, waits for them, and re-layouts  59.9 us
    all_gather x1, waiting for transfers between devices, per_device(): defect_full = lax.all_gather(defect, 'space', axis=0, tiled=True)  54.9 us
    ppermute x8, waiting for transfers between devices, extended(): lax.ppermute(lax.slice_in_dim(block, 0, width, axis=dim), axis, backward)  42 us
  transfers between devices with their start and end apart: 20, of which 18 were waited for; matrix products, arithmetic and copies ran while one was open for 2% of the time, Pallas kernels for 0%

profile of v1, /device:TPU:24, one launch (start us, length us, event | category | flops | bytes accessed | tf_op | source)
XLA Modules:
  0.0 822.0 jit_solution(13989459601107517006)
XLA Ops:
  7.6 4.6 collective-permute-start
  15.2 7.5 collective-permute-start.2
  25.2 3.9 collective-permute-done.2
  29.1 7.7 collective-permute-done.3
  40.2 3.9 collective-permute-start.5
  45.1 5.5 collective-permute-done.5
  54.8 3.9 collective-permute-start.7
  59.9 5.5 collective-permute-done.7
  67.1 7.9 collective-permute-done.8
  77.6 3.9 collective-permute-start.10
  84.1 4.1 collective-permute-done.10
  89.4 4.4 broadcast_in_dim.21
  95.1 24.8 %all-gather.5.cloned.1.call-done = f32[32,128,128]{2,1,0:T(8,128)} async-done(((f32[4,128,128]{2,1,0:T(8,128)}), f32[32,128,128]{2,1,0:T(8,128)}) %all-gather.5.cloned.1.call-update) | async-done | bytes 2097168 | tf_op jit(solution)/shard_map/all_gather | solution.py:54
  119.9 4.3 multiply_add_fusion
  124.2 54.9 %all-gather.3.cloned.1.call-done = f32[32,128,128]{2,1,0:T(8,128)} async-done(((f32[4,128,128]{2,1,0:T(8,128)}), f32[32,128,128]{2,1,0:T(8,128)}) %all-gather.3.cloned.1.call-update) | async-done | bytes 2097168 | tf_op jit(solution)/shard_map/all_gather | solution.py:88
  179.0 458.1 %while.17 = (s32[]{:T(128)}, f32[32,128,128]{2,1,0:T(8,128)}, f32[32,4,128,128]{3,2,1,0:T(8,128)}, f32[32,128,128]{2,1,0:T(8,128)}, f32[32,128,128]{2,1,0:T(8,12...) while((s32[]{:T(128)}, f32[32,128,128]{2,1,0:T(8,128)}, ...), condition=%wide.region_1.2_spmd, body=%wide.region_0.1_spmd.sunk | while | flops 12582929 | bytes 103285616 | solution.py:100
  179.0 2.9 fusion.209
  193.8 2.9 fusion.209
  223.4 2.9 fusion.209
  267.7 2.9 fusion.209
  297.2 2.9 fusion.209
  341.5 2.9 fusion.209
  356.3 2.9 fusion.209
  385.8 2.9 fusion.209
  400.6 2.9 fusion.209
  637.1 130.5 %reduce-scatter.2.cloned.1.call-done = f32[1,4,128,128]{3,2,1,0:T(8,128)} async-done(((f32[32,4,128,128]{3,2,1,0:T(8,128)}), f32[1,4,128,128]{3,2,1,0:T(8,128)}) %reduce-scatter.2.cloned.1.call-update) | async-done | bytes 262160 | tf_op jit(solution)/shard_map/reduce_scatter | solution.py:101
  768.7 4.7 collective-permute-start.11
  775.9 8.0 collective-permute-done.12
  788.5 3.9 collective-permute-start.14
  793.4 5.5 collective-permute-done.14
  802.5 3.9 collective-permute-start.16
  807.4 5.5 collective-permute-done.16
  (701 shorter events, 469.0 us)
Async XLA Ops:
  6.5 18.2 %copy-start.6 = (f32[1,4,128,128]{3,2,1,0:T(8,128)S(1)}, f32[1,4,128,128]{3,2,1,0:T(8,128)}, u32[]{:S(2)}) copy-start(f32[1,4,128,128]{3,2,1,0:T(8,128)} %param.7) | copy-start | bytes 786436
  6.5 113.3 %all-gather.5.cloned.1.call-start = ((), (), s32[]{:S(2)}) async-start(), calls=%async_computation.2 | async-start | bytes 2359296 | tf_op jit(solution)/shard_map/all_gather | solution.py:54
  7.6 17.1 %collective-permute-start = (f32[2,128,128]{2,1,0:T(8,128)S(1)}, f32[2,128,128]{2,1,0:T(8,128)S(1)}, u32[]{:S(2)}, u32[]{:S(2)}) collective-permute-start(f32[2,128,128]{2,1,0:T(8,128)S(1)} %get-tuple-element.351), channel_id=1, source_target_pairs={{0,1},{1,2},{2,3},{3,4},{4,5},{5,6},{6,7},{8,9},{9,10},{10,11},{11... | collective-permute-start | bytes 393224 | tf_op jit(solution)/shard_map/ppermute | solution.py:17
  12.2 12.5 %collective-permute-start.1 = (f32[2,128,128]{2,1,0:T(8,128)S(1)}, f32[2,128,128]{2,1,0:T(8,128)S(1)}, u32[]{:S(2)}, u32[]{:S(2)}) collective-permute-start(f32[2,128,128]{2,1,0:T(8,128)S(1)} %get-tuple-element.352), channel_id=1, source_target_pairs={{1,0},{2,1},{3,2},{4,3},{5,4},{6,5},{7,6},{9,8},{10,9},{11,10},{12... | collective-permute-start | bytes 393224 | tf_op jit(solution)/shard_map/ppermute | solution.py:20
  15.2 13.9 %collective-permute-start.2 = (f32[5,1,128,128]{3,2,1,0:T(8,128)S(1)}, f32[5,1,128,128]{3,2,1,0:T(8,128)S(1)}, u32[]{:S(2)}, u32[]{:S(2)}) collective-permute-start(f32[5,1,128,128]{3,2,1,0:T(8,128)S(1)} %get-tuple-element.237), channel_id=1, source_target_pairs={{0,1},{1,2},{2,3},{3,4},{4,5},{5,6},{6,7},{8,9},{9,10},{10,11},{11... | collective-permute-start | bytes 983048 | tf_op jit(solution)/shard_map/ppermute | solution.py:17
  22.7 14.1 %collective-permute-start.3 = (f32[5,1,128,128]{3,2,1,0:T(8,128)S(1)}, f32[5,1,128,128]{3,2,1,0:T(8,128)S(1)}, u32[]{:S(2)}, u32[]{:S(2)}) collective-permute-start(f32[5,1,128,128]{3,2,1,0:T(8,128)S(1)} %get-tuple-element.238), channel_id=1, source_target_pairs={{1,0},{2,1},{3,2},{4,3},{5,4},{6,5},{7,6},{9,8},{10,9},{11,10},{12... | collective-permute-start | bytes 983048 | tf_op jit(solution)/shard_map/ppermute | solution.py:20
  24.7 12.1 %copy-start.7 = (f32[4,4,128,128]{3,2,1,0:T(8,128)S(1)}, f32[4,4,128,128]{3,2,1,0:T(8,128)}, u32[]{:S(2)}) copy-start(f32[4,4,128,128]{3,2,1,0:T(8,128)} %param.5) | copy-start | bytes 3145732
  24.8 12.1 %copy-start.8 = (f32[4,128,128]{2,1,0:T(8,128)S(1)}, f32[4,128,128]{2,1,0:T(8,128)}, u32[]{:S(2)}) copy-start(f32[4,128,128]{2,1,0:T(8,128)} %param.6) | copy-start | bytes 786436
  37.0 51.6 %copy-start.4 = (f32[5,6,128,128]{3,2,1,0:T(8,128)}, f32[5,6,128,128]{3,2,1,0:T(8,128)S(1)}, u32[]{:S(2)}) copy-start(f32[5,6,128,128]{3,2,1,0:T(8,128)S(1)} %pad_maximum_fusion) | copy-start | bytes 5898244
  38.2 6.9 collective-permute-start.4
  40.2 10.5 %collective-permute-start.5 = (f32[2,128,128]{2,1,0:T(8,128)S(1)}, f32[2,128,128]{2,1,0:T(8,128)S(1)}, u32[]{:S(2)}, u32[]{:S(2)}) collective-permute-start(f32[2,128,128]{2,1,0:T(8,128)S(1)} %get-tuple-element.350), channel_id=1, source_target_pairs={{1,0},{2,1},{3,2},{4,3},{5,4},{6,5},{7,6},{9,8},{10,9},{11,10},{12... | collective-permute-start | bytes 393224 | tf_op jit(solution)/shard_map/ppermute | solution.py:20
  52.9 7.1 collective-permute-start.6
  54.8 10.7 %collective-permute-start.7 = (f32[2,128,128]{2,1,0:T(8,128)}, f32[2,128,128]{2,1,0:T(8,128)S(1)}, u32[]{:S(2)}, u32[]{:S(2)}) collective-permute-start(f32[2,128,128]{2,1,0:T(8,128)} %get-tuple-element.348), channel_id=1, source_target_pairs={{1,0},{2,1},{3,2},{4,3},{5,4},{6,5},{7,6},{9,8},{10,9},{11,10},{12... | collective-permute-start | bytes 393224 | tf_op jit(solution)/shard_map/ppermute | solution.py:20
  58.8 120.3 %all-gather.3.cloned.1.call-start = ((), (), s32[]{:S(2)}) async-start(), calls=%async_computation.1 | async-start | bytes 2359296 | tf_op jit(solution)/shard_map/all_gather | solution.py:88
  67.0 8.0 collective-permute-start.8
  75.7 8.3 %collective-permute-start.9 = (f32[2,128,128]{2,1,0:T(8,128)}, f32[2,128,128]{2,1,0:T(8,128)S(1)}, u32[]{:S(2)}, u32[]{:S(2)}) collective-permute-start(f32[2,128,128]{2,1,0:T(8,128)} %get-tuple-element.346), channel_id=1, source_target_pairs={{0,1},{1,2},{2,3},{3,4},{4,5},{5,6},{6,7},{8,9},{9,10},{10,11},{11... | collective-permute-start | bytes 393224 | tf_op jit(solution)/shard_map/ppermute | solution.py:17
  77.6 10.6 %collective-permute-start.10 = (f32[2,128,128]{2,1,0:T(8,128)S(1)}, f32[2,128,128]{2,1,0:T(8,128)S(1)}, u32[]{:S(2)}, u32[]{:S(2)}) collective-permute-start(f32[2,128,128]{2,1,0:T(8,128)S(1)} %get-tuple-element.345), channel_id=1, source_target_pairs={{1,0},{2,1},{3,2},{4,3},{5,4},{6,5},{7,6},{9,8},{10,9},{11,10},{12... | collective-permute-start | bytes 393224 | tf_op jit(solution)/shard_map/ppermute | solution.py:20
  94.9 672.8 %reduce-scatter.2.cloned.1.call-start = ((), (), s32[]{:S(2)}) async-start(), calls=%async_computation.3 | async-start | bytes 8650752 | tf_op jit(solution)/shard_map/reduce_scatter | solution.py:101
  179.0 2.9 copy-start
  193.8 2.9 copy-start
  208.6 2.9 copy-start
  223.4 2.9 copy-start
  238.1 2.9 copy-start
  252.9 2.9 copy-start
  267.7 2.9 copy-start
  768.7 7.3 collective-permute-start.11
  773.4 10.5 %collective-permute-start.12 = (f32[2,128,128]{2,1,0:T(8,128)S(1)}, f32[2,128,128]{2,1,0:T(8,128)S(1)}, u32[]{:S(2)}, u32[]{:S(2)}) collective-permute-start(f32[2,128,128]{2,1,0:T(8,128)S(1)} %get-tuple-element.344), channel_id=1, source_target_pairs={{1,0},{2,1},{3,2},{4,3},{5,4},{6,5},{7,6},{9,8},{10,9},{11,10},{12... | collective-permute-start | bytes 393224 | tf_op jit(solution)/shard_map/ppermute | solution.py:20
  786.6 6.9 collective-permute-start.13
  788.5 10.5 %collective-permute-start.14 = (f32[2,128,128]{2,1,0:T(8,128)S(1)}, f32[2,128,128]{2,1,0:T(8,128)S(1)}, u32[]{:S(2)}, u32[]{:S(2)}) collective-permute-start(f32[2,128,128]{2,1,0:T(8,128)S(1)} %get-tuple-element.342), channel_id=1, source_target_pairs={{1,0},{2,1},{3,2},{4,3},{5,4},{6,5},{7,6},{9,8},{10,9},{11,10},{12... | collective-permute-start | bytes 393224 | tf_op jit(solution)/shard_map/ppermute | solution.py:20
  800.2 6.2 copy-start.9
  800.5 6.9 collective-permute-start.15
  802.5 10.5 %collective-permute-start.16 = (f32[2,128,128]{2,1,0:T(8,128)S(1)}, f32[2,128,128]{2,1,0:T(8,128)S(1)}, u32[]{:S(2)}, u32[]{:S(2)}) collective-permute-start(f32[2,128,128]{2,1,0:T(8,128)S(1)} %get-tuple-element.340), channel_id=1, source_target_pairs={{1,0},{2,1},{3,2},{4,3},{5,4},{6,5},{7,6},{9,8},{10,9},{11,10},{12... | collective-permute-start | bytes 393224 | tf_op jit(solution)/shard_map/ppermute | solution.py:20
  (118 other events, 233.0 us)
Sparse Core Ops, SparseCore 0:
  58.9 60.9 all-gather.4
  122.5 56.4 all-gather.2
  637.2 130.3 reduce-scatter.1

commit v2 on v0

--- a/solution.py
+++ b/solution.py
@@ -1,6 +1,10 @@
+import functools
+
 import jax
 import jax.numpy as jnp
 from jax import lax
+from jax.experimental import pallas as pl
+from jax.experimental.pallas import tpu as pltpu
 from jax.sharding import PartitionSpec as P
 
 CF = 4
@@ -39,14 +43,108 @@
     return (target + weight * neighbours(field)) / scaled
 
 
+def column_slabs(slab, lag):
+    n_tm = lax.axis_size("tm")
+    n_sp = lax.axis_size("space")
+    slots = []
+    for t in range(n_sp):
+        if t == 0 and lag == 0:
+            slots.append(slab)
+            continue
+        pairs = []
+        for k in range(n_tm):
+            for q in range(n_sp):
+                pairs.append((k * n_sp + q, ((k + lag) % n_tm) * n_sp + (q + t) % n_sp))
+        slots.append(lax.ppermute(slab, ("tm", "space"), pairs))
+    return jnp.stack(slots, axis=0)
+
+
+def coarse_kernel(place_ref, slots_ref, w_ref, s_ref, o_ref, a_buf, b_buf):
+    n_sp, depth, rows, cols = slots_ref.shape
+    planes = n_sp * depth
+    me = place_ref[0]
+    power = place_ref[1]
+    zero = jnp.zeros((rows, cols), jnp.float32)
+    a_buf[0] = zero
+    a_buf[planes + 1] = zero
+    b_buf[0] = zero
+    b_buf[planes + 1] = zero
+
+    def load(q, carry):
+        slot = lax.rem(me - q + n_sp, n_sp)
+        for p in range(depth):
+            a_buf[1 + q * depth + p] = slots_ref[slot, p]
+        return carry
+
+    lax.fori_loop(0, n_sp, load, 0)
+
+    def sweep(src, dst, z):
+        centre = src[z + 1]
+        total = src[z] + src[z + 2]
+        total = total + pltpu.roll(centre, 1, 0) + pltpu.roll(centre, rows - 1, 0)
+        total = total + pltpu.roll(centre, 1, 1) + pltpu.roll(centre, cols - 1, 1)
+        dst[z + 1] = (a_buf[z + 1] + w_ref[z] * total) / s_ref[z]
+
+    def first(z, carry):
+        sweep(a_buf, b_buf, z)
+        return carry
+
+    def second(z, carry):
+        sweep(b_buf, a_buf, z)
+        return carry
+
+    def one(i, carry):
+        lax.fori_loop(0, planes, first, 0)
+        lax.fori_loop(0, planes, second, 0)
+        return carry
+
+    lax.fori_loop(0, power, one, 0)
+    for p in range(depth):
+        o_ref[p] = a_buf[1 + me * depth + p]
+
+
+def coarse_power(power, place, slots, weight, scaled):
+    n_sp, depth, rows, cols = slots.shape
+    planes = n_sp * depth
+    vmem = pltpu.MemorySpace.VMEM if hasattr(pltpu, "MemorySpace") else pltpu.VMEM
+    return pl.pallas_call(
+        coarse_kernel,
+        out_shape=jax.ShapeDtypeStruct((depth, rows, cols), jnp.float32),
+        in_specs=[
+            pl.BlockSpec(memory_space=pltpu.SMEM),
+            pl.BlockSpec(memory_space=vmem),
+            pl.BlockSpec(memory_space=vmem),
+            pl.BlockSpec(memory_space=vmem),
+        ],
+        out_specs=pl.BlockSpec(memory_space=vmem),
+        scratch_shapes=[
+            pltpu.VMEM((planes + 2, rows, cols), jnp.float32),
+            pltpu.VMEM((planes + 2, rows, cols), jnp.float32),
+        ],
+        compiler_params=pltpu.CompilerParams(vmem_limit_bytes=48 * 1024 * 1024),
+        cost_estimate=pl.CostEstimate(
+            flops=2 * power * planes * rows * cols * 12,
+            bytes_accessed=4 * planes * rows * cols * 3,
+            transcendentals=0,
+        ),
+    )(jnp.stack([place, jnp.int32(power)]), slots, weight, scaled)
+
+
 def per_device(forcing, conductivity, guess):
     stacked = jnp.concatenate([conductivity[None], forcing], axis=0)
     widened = extended(stacked, (("space", 1),), 1)
     kappa_wide = widened[0]
     fine_weight = step_length * kappa_wide
     fine_scaled = 1.0 + 6.0 * fine_weight
-    coarse_weight = CF * step_length * kappa_wide
+
+    n_sp = lax.axis_size("space")
+    me_sp = lax.axis_index("space")
+    order = lax.rem(me_sp - jnp.arange(n_sp, dtype=jnp.int32) + n_sp, n_sp)
+    kappa_full = jnp.take(column_slabs(conductivity, 0), order, axis=0)
+    kappa_full = kappa_full.reshape((-1,) + conductivity.shape[1:])
+    coarse_weight = CF * step_length * kappa_full
     coarse_scaled = 1.0 + 6.0 * coarse_weight
+    place = me_sp.astype(jnp.int32)
 
     def advance(state, weight, scaled, source):
         padded = extended(state, (("space", 0),), 2)
@@ -59,9 +157,6 @@
     def fine_step(state, index):
         return advance(state, fine_weight, fine_scaled, widened[1 + index])
 
-    def coarse_step(state):
-        return advance(state, coarse_weight, coarse_scaled, None)
-
     def relax(anchor):
         states = [anchor]
         for index in range(1, CF):
@@ -72,13 +167,14 @@
     states = relax(anchor)
     before = shifted(states[-1], "tm", 1)
     defect = fine_step(before, 0) - anchor
+
     count = lax.axis_size("tm")
-
-    def relay(turn, carried):
-        moved = shifted(carried, "tm", 1)
-        return defect + coarse_step(moved)
-
-    total = lax.fori_loop(0, count - 1, relay, defect)
+    total = defect
+    lag = 1
+    while lag < count:
+        slots = column_slabs(total, lag)
+        total = total + coarse_power(lag, place, slots, coarse_weight, coarse_scaled)
+        lag *= 2
     anchor = anchor + total
     return jnp.stack(relax(anchor), axis=0)
 

time: 840 us -> 746 us (0.89)
  waiting for transfers between devices: 507 us -> 209 us
  Pallas kernels: 0 us -> 217 us
  starting transfers between devices: 242 us -> 278 us
  local copies, waits for them, and re-layouts: 53.6 us -> 21.1 us
  other arithmetic: 30.7 us -> 10.8 us
    ppermute x32 -> x1, waiting for transfers between devices: 253 us -> 6.45 us  [shifted(): return lax.ppermute(value, axis, pairs)]
    ppermute x0 -> x47, starting transfers between devices: none -> 225 us  [column_slabs(): slots.append(lax.ppermute(slab, ('tm', 'space'), pairs))]
    pallas_call x0 -> x5, Pallas kernels: none -> 217 us  [coarse_power(): pl.pallas_call(coarse_kernel, out_shape=jax.ShapeDtypeStruct((depth, rows...]
    ppermute x39 -> x8, waiting for transfers between devices: 206 us -> 45.5 us  [extended(): lax.ppermute(lax.slice_in_dim(block, 0, width, axis=dim), axis, backward)]
    ppermute x0 -> x47, waiting for transfers between devices: none -> 141 us  [column_slabs(): slots.append(lax.ppermute(slab, ('tm', 'space'), pairs))]
    ppermute x39 -> x8, starting transfers between devices: 145 us -> 25.9 us  [extended(): lax.ppermute(lax.slice_in_dim(block, 0, width, axis=dim), axis, backward)]
    ppermute x39 -> x8, starting transfers between devices: 94.4 us -> 26.4 us  [extended(): lax.ppermute(lax.slice_in_dim(block, block.shape[dim] - width, None, axis...]
    ppermute x39 -> x8, waiting for transfers between devices: 47.8 us -> 16 us  [extended(): lax.ppermute(lax.slice_in_dim(block, block.shape[dim] - width, None, axis...]
  transfers between devices with their start and end apart: 110 -> 64, of which waited for: 108 -> 39; matrix products, arithmetic and copies ran while one was open for 0% -> 3% of each run, Pallas kernels for 0% -> 0%
where the time goes in v2:
time: 746 us; the launch traced here: 738 us
  starting transfers between devices  278 us (37%)
  Pallas kernels  217 us (29%)
  waiting for transfers between devices  209 us (28%)
  local copies, waits for them, and re-layouts  21.1 us (3%)
  other arithmetic  10.8 us (1%)
    ppermute x47, starting transfers between devices, column_slabs(): slots.append(lax.ppermute(slab, ('tm', 'space'), pairs))  225 us
    pallas_call x5, Pallas kernels, coarse_power(): pl.pallas_call(coarse_kernel, out_shape=jax.ShapeDtypeStruct((depth, rows...  217 us
    ppermute x47, waiting for transfers between devices, column_slabs(): slots.append(lax.ppermute(slab, ('tm', 'space'), pairs))  141 us
    ppermute x8, waiting for transfers between devices, extended(): lax.ppermute(lax.slice_in_dim(block, 0, width, axis=dim), axis, backward)  45.5 us
    ppermute x8, starting transfers between devices, extended(): lax.ppermute(lax.slice_in_dim(block, block.shape[dim] - width, None, axis...  26.4 us
    ppermute x8, starting transfers between devices, extended(): lax.ppermute(lax.slice_in_dim(block, 0, width, axis=dim), axis, backward)  25.9 us
    ppermute x8, waiting for transfers between devices, extended(): lax.ppermute(lax.slice_in_dim(block, block.shape[dim] - width, None, axis...  16 us
  transfers between devices with their start and end apart: 64, of which 39 were waited for; matrix products, arithmetic and copies ran while one was open for 3% of the time, Pallas kernels for 0%

profile of v2, /device:TPU:24, one launch (start us, length us, event | category | flops | bytes accessed | tf_op | source)
XLA Modules:
  0.0 737.5 jit_solution(1273245251689712199)
XLA Ops:
  16.3 10.9 %collective-permute-done = f32[2,128,128]{2,1,0:T(8,128)S(1)} collective-permute-done((f32[2,128,128]{2,1,0:T(8,128)S(1)}, f32[2,128,128]{2,1,0:T(8,128)S(1)}, u32[]{:S(2)}, u32[]{:S(2)}) %collective-permute-start) | collective-permute-done | bytes 131104 | tf_op jit(solution)/shard_map/ppermute | solution.py:21
  27.3 8.1 %collective-permute-start.2 = (f32[5,1,128,128]{3,2,1,0:T(8,128)S(1)}, f32[5,1,128,128]{3,2,1,0:T(8,128)S(1)}, u32[]{:S(2)}, u32[]{:S(2)}) collective-permute-start(f32[5,1,128,128]{3,2,1,0:T(8,128)S(1)} %get-tuple-element.23), channel_id=1, source_target_pairs={{0,1},{1,2},{2,3},{3,4},{4,5},{5,6},{6,7},{8,9},{9,10},{10,11},{11... | collective-permute-start | bytes 983048 | tf_op jit(solution)/shard_map/ppermute | solution.py:21
  42.6 11.6 %collective-permute-done.3 = f32[5,1,128,128]{3,2,1,0:T(8,128)S(1)} collective-permute-done((f32[5,1,128,128]{3,2,1,0:T(8,128)S(1)}, f32[5,1,128,128]{3,2,1,0:T(8,128)S(1)}, u32[]{:S(2)}, u32[]{:S(2)}) %collective-permute-start.3) | collective-permute-done | bytes 327712 | tf_op jit(solution)/shard_map/ppermute | solution.py:24
  85.7 6.5 collective-permute-done.8
  139.5 6.9 collective-permute-done.18
  146.5 8.5 %shard_map.37 = f32[4,128,128]{2,1,0:T(8,128)S(1)} custom-call(s32[2]{0:T(128)S(1)} %pad_add_fusion.place_ref, f32[8,4,128,128]{3,2,1,0:T(8,128)S(1)} %bitcast_dynamic-update-slice_fusion.39.slots_ref, f32[32,128,128]{2,1,0:T(8,128)S(1)} %get-tuple-element.20.w_ref, f32[32,128,128]{2,1,0:T(8,128)} %get-tuple-element.19.s_ref), custom_call_target="tpu_custom_call" | custom-call | flops 12582912 | bytes 6291456 | tf_op jit(solution)/shard_map/pallas_call | solution.py:110
  158.3 6.6 collective-permute-start.29
  182.9 10.7 %collective-permute-done.30 = f32[4,128,128]{2,1,0:T(8,128)S(1)} collective-permute-done((f32[4,128,128]{2,1,0:T(8,128)S(1)}, f32[4,128,128]{2,1,0:T(8,128)S(1)}, u32[]{:S(2)}, u32[]{:S(2)}) %collective-permute-start.30) | collective-permute-done | bytes 262176 | tf_op jit(solution)/shard_map/ppermute | solution.py:58
  194.3 6.8 collective-permute-done.32
  204.3 15.3 %shard_map.38 = f32[4,128,128]{2,1,0:T(8,128)S(1)} custom-call(s32[2]{0:T(128)S(1)} %pad_add_fusion.1.place_ref, f32[8,4,128,128]{3,2,1,0:T(8,128)S(1)} %bitcast_dynamic-update-slice_fusion.24.slots_ref, f32[32,128,128]{2,1,0:T(8,128)S(1)} %get-tuple-element.20.w_ref, f32[32,128,128]{2,1,0:T(8,128)} %get-tuple-element.19.s_ref), custom_call_target="tpu_custom_call" | custom-call | flops 25165824 | bytes 6291456 | tf_op jit(solution)/shard_map/pallas_call | solution.py:110
  228.5 14.7 %collective-permute-start.36 = (f32[4,128,128]{2,1,0:T(8,128)S(1)}, f32[4,128,128]{2,1,0:T(8,128)S(1)}, u32[]{:S(2)}, u32[]{:S(2)}) collective-permute-start(f32[4,128,128]{2,1,0:T(8,128)S(1)} %add.397), channel_id=1, source_target_pairs={{0,34},{1,35},{2,36},{3,37},{4,38},{5,39},{6,32},{7,33},{8,42},{9,... | collective-permute-start | bytes 786440 | tf_op jit(solution)/shard_map/ppermute | solution.py:58
  251.7 7.3 collective-permute-done.36
  259.8 6.9 collective-permute-done.38
  266.8 11.0 %collective-permute-done.39 = f32[4,128,128]{2,1,0:T(8,128)S(1)} collective-permute-done((f32[4,128,128]{2,1,0:T(8,128)S(1)}, f32[4,128,128]{2,1,0:T(8,128)S(1)}, u32[]{:S(2)}, u32[]{:S(2)}) %collective-permute-start.39) | collective-permute-done | bytes 262176 | tf_op jit(solution)/shard_map/ppermute | solution.py:58
  282.6 28.7 %shard_map.39 = f32[4,128,128]{2,1,0:T(8,128)S(1)} custom-call(s32[2]{0:T(128)S(1)} %pad_add_fusion.2.place_ref, f32[8,4,128,128]{3,2,1,0:T(8,128)S(1)} %bitcast_dynamic-update-slice_fusion.16.slots_ref, f32[32,128,128]{2,1,0:T(8,128)S(1)} %get-tuple-element.20.w_ref, f32[32,128,128]{2,1,0:T(8,128)} %get-tuple-element.19.s_ref), custom_call_target="tpu_custom_call" | custom-call | flops 50331648 | bytes 6291456 | tf_op jit(solution)/shard_map/pallas_call | solution.py:110
  325.7 9.7 %collective-permute-start.45 = (f32[4,128,128]{2,1,0:T(8,128)S(1)}, f32[4,128,128]{2,1,0:T(8,128)S(1)}, u32[]{:S(2)}, u32[]{:S(2)}) collective-permute-start(f32[4,128,128]{2,1,0:T(8,128)S(1)} %add.398), channel_id=1, source_target_pairs={{0,67},{1,68},{2,69},{3,70},{4,71},{5,64},{6,65},{7,66},{8,75},{9,... | collective-permute-start | bytes 786440 | tf_op jit(solution)/shard_map/ppermute | solution.py:58
  335.4 11.8 %collective-permute-start.46 = (f32[4,128,128]{2,1,0:T(8,128)S(1)}, f32[4,128,128]{2,1,0:T(8,128)S(1)}, u32[]{:S(2)}, u32[]{:S(2)}) collective-permute-start(f32[4,128,128]{2,1,0:T(8,128)S(1)} %add.398), channel_id=1, source_target_pairs={{0,68},{1,69},{2,70},{3,71},{4,64},{5,65},{6,66},{7,67},{8,76},{9,... | collective-permute-start | bytes 786440 | tf_op jit(solution)/shard_map/ppermute | solution.py:58
  347.2 12.1 %collective-permute-start.47 = (f32[4,128,128]{2,1,0:T(8,128)S(1)}, f32[4,128,128]{2,1,0:T(8,128)S(1)}, u32[]{:S(2)}, u32[]{:S(2)}) collective-permute-start(f32[4,128,128]{2,1,0:T(8,128)S(1)} %add.398), channel_id=1, source_target_pairs={{0,69},{1,70},{2,71},{3,64},{4,65},{5,66},{6,67},{7,68},{8,77},{9,... | collective-permute-start | bytes 786440 | tf_op jit(solution)/shard_map/ppermute | solution.py:58
  359.4 11.9 %collective-permute-start.48 = (f32[4,128,128]{2,1,0:T(8,128)S(1)}, f32[4,128,128]{2,1,0:T(8,128)S(1)}, u32[]{:S(2)}, u32[]{:S(2)}) collective-permute-start(f32[4,128,128]{2,1,0:T(8,128)S(1)} %add.398), channel_id=1, source_target_pairs={{0,70},{1,71},{2,64},{3,65},{4,66},{5,67},{6,68},{7,69},{8,78},{9,... | collective-permute-start | bytes 786440 | tf_op jit(solution)/shard_map/ppermute | solution.py:58
  371.4 11.9 %collective-permute-start.49 = (f32[4,128,128]{2,1,0:T(8,128)S(1)}, f32[4,128,128]{2,1,0:T(8,128)S(1)}, u32[]{:S(2)}, u32[]{:S(2)}) collective-permute-start(f32[4,128,128]{2,1,0:T(8,128)S(1)} %add.398), channel_id=1, source_target_pairs={{0,71},{1,64},{2,65},{3,66},{4,67},{5,68},{6,69},{7,70},{8,79},{9,... | collective-permute-start | bytes 786440 | tf_op jit(solution)/shard_map/ppermute | solution.py:58
  385.7 22.9 %collective-permute-done.48 = f32[4,128,128]{2,1,0:T(8,128)S(1)} collective-permute-done((f32[4,128,128]{2,1,0:T(8,128)S(1)}, f32[4,128,128]{2,1,0:T(8,128)S(1)}, u32[]{:S(2)}, u32[]{:S(2)}) %collective-permute-start.48) | collective-permute-done | bytes 262176 | tf_op jit(solution)/shard_map/ppermute | solution.py:58
  411.8 55.6 %shard_map.40 = f32[4,128,128]{2,1,0:T(8,128)S(1)} custom-call(s32[2]{0:T(128)S(1)} %pad_add_fusion.3.place_ref, f32[8,4,128,128]{3,2,1,0:T(8,128)S(1)} %bitcast_dynamic-update-slice_fusion.8.slots_ref, f32[32,128,128]{2,1,0:T(8,128)S(1)} %get-tuple-element.20.w_ref, f32[32,128,128]{2,1,0:T(8,128)} %get-tuple-element.19.s_ref), custom_call_target="tpu_custom_call" | custom-call | flops 100663296 | bytes 6291456 | tf_op jit(solution)/shard_map/pallas_call | solution.py:110
  467.5 8.4 %collective-permute-start.50 = (f32[4,128,128]{2,1,0:T(8,128)S(1)}, f32[4,128,128]{2,1,0:T(8,128)S(1)}, u32[]{:S(2)}, u32[]{:S(2)}) collective-permute-start(f32[4,128,128]{2,1,0:T(8,128)S(1)} %add.399), channel_id=1, source_target_pairs={{0,128},{1,129},{2,130},{3,131},{4,132},{5,133},{6,134},{7,135},{8... | collective-permute-start | bytes 786440 | tf_op jit(solution)/shard_map/ppermute | solution.py:58
  475.9 11.8 %collective-permute-start.51 = (f32[4,128,128]{2,1,0:T(8,128)S(1)}, f32[4,128,128]{2,1,0:T(8,128)S(1)}, u32[]{:S(2)}, u32[]{:S(2)}) collective-permute-start(f32[4,128,128]{2,1,0:T(8,128)S(1)} %add.399), channel_id=1, source_target_pairs={{0,129},{1,130},{2,131},{3,132},{4,133},{5,134},{6,135},{7,128},{8... | collective-permute-start | bytes 786440 | tf_op jit(solution)/shard_map/ppermute | solution.py:58
  487.8 11.9 %collective-permute-start.52 = (f32[4,128,128]{2,1,0:T(8,128)S(1)}, f32[4,128,128]{2,1,0:T(8,128)S(1)}, u32[]{:S(2)}, u32[]{:S(2)}) collective-permute-start(f32[4,128,128]{2,1,0:T(8,128)S(1)} %add.399), channel_id=1, source_target_pairs={{0,130},{1,131},{2,132},{3,133},{4,134},{5,135},{6,128},{7,129},{8... | collective-permute-start | bytes 786440 | tf_op jit(solution)/shard_map/ppermute | solution.py:58
  499.6 11.8 %collective-permute-start.53 = (f32[4,128,128]{2,1,0:T(8,128)S(1)}, f32[4,128,128]{2,1,0:T(8,128)S(1)}, u32[]{:S(2)}, u32[]{:S(2)}) collective-permute-start(f32[4,128,128]{2,1,0:T(8,128)S(1)} %add.399), channel_id=1, source_target_pairs={{0,131},{1,132},{2,133},{3,134},{4,135},{5,128},{6,129},{7,130},{8... | collective-permute-start | bytes 786440 | tf_op jit(solution)/shard_map/ppermute | solution.py:58
  511.5 11.8 %collective-permute-start.54 = (f32[4,128,128]{2,1,0:T(8,128)S(1)}, f32[4,128,128]{2,1,0:T(8,128)S(1)}, u32[]{:S(2)}, u32[]{:S(2)}) collective-permute-start(f32[4,128,128]{2,1,0:T(8,128)S(1)} %add.399), channel_id=1, source_target_pairs={{0,132},{1,133},{2,134},{3,135},{4,128},{5,129},{6,130},{7,131},{8... | collective-permute-start | bytes 786440 | tf_op jit(solution)/shard_map/ppermute | solution.py:58
  523.3 11.8 %collective-permute-start.55 = (f32[4,128,128]{2,1,0:T(8,128)S(1)}, f32[4,128,128]{2,1,0:T(8,128)S(1)}, u32[]{:S(2)}, u32[]{:S(2)}) collective-permute-start(f32[4,128,128]{2,1,0:T(8,128)S(1)} %add.399), channel_id=1, source_target_pairs={{0,133},{1,134},{2,135},{3,128},{4,129},{5,130},{6,131},{7,132},{8... | collective-permute-start | bytes 786440 | tf_op jit(solution)/shard_map/ppermute | solution.py:58
  535.2 11.9 %collective-permute-start.56 = (f32[4,128,128]{2,1,0:T(8,128)S(1)}, f32[4,128,128]{2,1,0:T(8,128)S(1)}, u32[]{:S(2)}, u32[]{:S(2)}) collective-permute-start(f32[4,128,128]{2,1,0:T(8,128)S(1)} %add.399), channel_id=1, source_target_pairs={{0,134},{1,135},{2,128},{3,129},{4,130},{5,131},{6,132},{7,133},{8... | collective-permute-start | bytes 786440 | tf_op jit(solution)/shard_map/ppermute | solution.py:58
  547.1 11.9 %collective-permute-start.57 = (f32[4,128,128]{2,1,0:T(8,128)S(1)}, f32[4,128,128]{2,1,0:T(8,128)S(1)}, u32[]{:S(2)}, u32[]{:S(2)}) collective-permute-start(f32[4,128,128]{2,1,0:T(8,128)S(1)} %add.399), channel_id=1, source_target_pairs={{0,135},{1,128},{2,129},{3,130},{4,131},{5,132},{6,133},{7,134},{8... | collective-permute-start | bytes 786440 | tf_op jit(solution)/shard_map/ppermute | solution.py:58
  563.6 20.0 %collective-permute-done.57 = f32[4,128,128]{2,1,0:T(8,128)S(1)} collective-permute-done((f32[4,128,128]{2,1,0:T(8,128)S(1)}, f32[4,128,128]{2,1,0:T(8,128)S(1)}, u32[]{:S(2)}, u32[]{:S(2)}) %collective-permute-start.57) | collective-permute-done | bytes 262176 | tf_op jit(solution)/shard_map/ppermute | solution.py:58
  583.6 109.4 %shard_map.41 = f32[4,128,128]{2,1,0:T(8,128)S(1)} custom-call(s32[2]{0:T(128)S(1)} %pad_add_fusion.4.place_ref, f32[8,4,128,128]{3,2,1,0:T(8,128)S(1)} %bitcast_dynamic-update-slice_fusion.slots_ref, f32[32,128,128]{2,1,0:T(8,128)S(1)} %get-tuple-element.20.w_ref, f32[32,128,128]{2,1,0:T(8,128)} %get-tuple-element.19.s_ref), custom_call_target="tpu_custom_call" | custom-call | flops 201326592 | bytes 6291456 | tf_op jit(solution)/shard_map/pallas_call | solution.py:110
  (260 shorter events, 218.7 us)
Async XLA Ops:
  0.0 35.9 %collective-permute-start.19 = (f32[4,128,128]{2,1,0:T(8,128)}, f32[4,128,128]{2,1,0:T(8,128)S(1)}, u32[]{:S(2)}, u32[]{:S(2)}) collective-permute-start(f32[4,128,128]{2,1,0:T(8,128)} %param.4), channel_id=1, source_target_pairs={{0,1},{1,2},{2,3},{3,4},{4,5},{5,6},{6,7},{7,0},{8,9},{9,10},{10,1... | collective-permute-start | bytes 786440 | tf_op jit(solution)/shard_map/ppermute | solution.py:58
  2.7 36.0 %collective-permute-start.20 = (f32[4,128,128]{2,1,0:T(8,128)}, f32[4,128,128]{2,1,0:T(8,128)S(1)}, u32[]{:S(2)}, u32[]{:S(2)}) collective-permute-start(f32[4,128,128]{2,1,0:T(8,128)} %param.4), channel_id=1, source_target_pairs={{0,2},{1,3},{2,4},{3,5},{4,6},{5,7},{6,0},{7,1},{8,10},{9,11},{10,... | collective-permute-start | bytes 786440 | tf_op jit(solution)/shard_map/ppermute | solution.py:58
  5.3 52.2 %collective-permute-start.21 = (f32[4,128,128]{2,1,0:T(8,128)}, f32[4,128,128]{2,1,0:T(8,128)}, u32[]{:S(2)}, u32[]{:S(2)}) collective-permute-start(f32[4,128,128]{2,1,0:T(8,128)} %param.4), channel_id=1, source_target_pairs={{0,3},{1,4},{2,5},{3,6},{4,7},{5,0},{6,1},{7,2},{8,11},{9,12},{10,... | collective-permute-start | bytes 786440 | tf_op jit(solution)/shard_map/ppermute | solution.py:58
  27.3 44.9 %collective-permute-start.22 = (f32[4,128,128]{2,1,0:T(8,128)S(1)}, f32[4,128,128]{2,1,0:T(8,128)S(1)}, u32[]{:S(2)}, u32[]{:S(2)}) collective-permute-start(f32[4,128,128]{2,1,0:T(8,128)S(1)} %copy-done.3), channel_id=1, source_target_pairs={{0,4},{1,5},{2,6},{3,7},{4,0},{5,1},{6,2},{7,3},{8,12},{9,13},{10,... | collective-permute-start | bytes 786440 | tf_op jit(solution)/shard_map/ppermute | solution.py:58
  38.7 45.6 %collective-permute-start.23 = (f32[4,128,128]{2,1,0:T(8,128)S(1)}, f32[4,128,128]{2,1,0:T(8,128)S(1)}, u32[]{:S(2)}, u32[]{:S(2)}) collective-permute-start(f32[4,128,128]{2,1,0:T(8,128)S(1)} %copy-done.3), channel_id=1, source_target_pairs={{0,5},{1,6},{2,7},{3,0},{4,1},{5,2},{6,3},{7,4},{8,13},{9,14},{10,... | collective-permute-start | bytes 786440 | tf_op jit(solution)/shard_map/ppermute | solution.py:58
  40.8 44.2 %collective-permute-start.24 = (f32[4,128,128]{2,1,0:T(8,128)S(1)}, f32[4,128,128]{2,1,0:T(8,128)S(1)}, u32[]{:S(2)}, u32[]{:S(2)}) collective-permute-start(f32[4,128,128]{2,1,0:T(8,128)S(1)} %copy-done.3), channel_id=1, source_target_pairs={{0,6},{1,7},{2,0},{3,1},{4,2},{5,3},{6,4},{7,5},{8,14},{9,15},{10,... | collective-permute-start | bytes 786440 | tf_op jit(solution)/shard_map/ppermute | solution.py:58
  63.1 31.7 %collective-permute-start.25 = (f32[4,128,128]{2,1,0:T(8,128)S(1)}, f32[4,128,128]{2,1,0:T(8,128)S(1)}, u32[]{:S(2)}, u32[]{:S(2)}) collective-permute-start(f32[4,128,128]{2,1,0:T(8,128)S(1)} %copy-done.3), channel_id=1, source_target_pairs={{0,7},{1,0},{2,1},{3,2},{4,3},{5,4},{6,5},{7,6},{8,15},{9,8},{10,9... | collective-permute-start | bytes 786440 | tf_op jit(solution)/shard_map/ppermute | solution.py:58
  164.9 28.7 %collective-permute-start.30 = (f32[4,128,128]{2,1,0:T(8,128)S(1)}, f32[4,128,128]{2,1,0:T(8,128)S(1)}, u32[]{:S(2)}, u32[]{:S(2)}) collective-permute-start(f32[4,128,128]{2,1,0:T(8,128)S(1)} %add.396), channel_id=1, source_target_pairs={{0,20},{1,21},{2,22},{3,23},{4,16},{5,17},{6,18},{7,19},{8,28},{9,... | collective-permute-start | bytes 786440 | tf_op jit(solution)/shard_map/ppermute | solution.py:58
  166.6 27.6 %collective-permute-start.31 = (f32[4,128,128]{2,1,0:T(8,128)S(1)}, f32[4,128,128]{2,1,0:T(8,128)S(1)}, u32[]{:S(2)}, u32[]{:S(2)}) collective-permute-start(f32[4,128,128]{2,1,0:T(8,128)S(1)} %add.396), channel_id=1, source_target_pairs={{0,21},{1,22},{2,23},{3,16},{4,17},{5,18},{6,19},{7,20},{8,29},{9,... | collective-permute-start | bytes 786440 | tf_op jit(solution)/shard_map/ppermute | solution.py:58
  174.6 26.5 %collective-permute-start.32 = (f32[4,128,128]{2,1,0:T(8,128)S(1)}, f32[4,128,128]{2,1,0:T(8,128)S(1)}, u32[]{:S(2)}, u32[]{:S(2)}) collective-permute-start(f32[4,128,128]{2,1,0:T(8,128)S(1)} %add.396), channel_id=1, source_target_pairs={{0,22},{1,23},{2,16},{3,17},{4,18},{5,19},{6,20},{7,21},{8,30},{9,... | collective-permute-start | bytes 786440 | tf_op jit(solution)/shard_map/ppermute | solution.py:58
  178.8 25.4 %collective-permute-start.33 = (f32[4,128,128]{2,1,0:T(8,128)S(1)}, f32[4,128,128]{2,1,0:T(8,128)S(1)}, u32[]{:S(2)}, u32[]{:S(2)}) collective-permute-start(f32[4,128,128]{2,1,0:T(8,128)S(1)} %add.396), channel_id=1, source_target_pairs={{0,23},{1,16},{2,17},{3,18},{4,19},{5,20},{6,21},{7,22},{8,31},{9,... | collective-permute-start | bytes 786440 | tf_op jit(solution)/shard_map/ppermute | solution.py:58
  219.6 25.6 %collective-permute-start.34 = (f32[4,128,128]{2,1,0:T(8,128)S(1)}, f32[4,128,128]{2,1,0:T(8,128)S(1)}, u32[]{:S(2)}, u32[]{:S(2)}) collective-permute-start(f32[4,128,128]{2,1,0:T(8,128)S(1)} %add.397), channel_id=1, source_target_pairs={{0,32},{1,33},{2,34},{3,35},{4,36},{5,37},{6,38},{7,39},{8,40},{9,... | collective-permute-start | bytes 786440 | tf_op jit(solution)/shard_map/ppermute | solution.py:58
  222.8 24.6 %collective-permute-start.35 = (f32[4,128,128]{2,1,0:T(8,128)S(1)}, f32[4,128,128]{2,1,0:T(8,128)S(1)}, u32[]{:S(2)}, u32[]{:S(2)}) collective-permute-start(f32[4,128,128]{2,1,0:T(8,128)S(1)} %add.397), channel_id=1, source_target_pairs={{0,33},{1,34},{2,35},{3,36},{4,37},{5,38},{6,39},{7,32},{8,41},{9,... | collective-permute-start | bytes 786440 | tf_op jit(solution)/shard_map/ppermute | solution.py:58
  228.5 30.5 %collective-permute-start.36 = (f32[4,128,128]{2,1,0:T(8,128)S(1)}, f32[4,128,128]{2,1,0:T(8,128)S(1)}, u32[]{:S(2)}, u32[]{:S(2)}) collective-permute-start(f32[4,128,128]{2,1,0:T(8,128)S(1)} %add.397), channel_id=1, source_target_pairs={{0,34},{1,35},{2,36},{3,37},{4,38},{5,39},{6,32},{7,33},{8,42},{9,... | collective-permute-start | bytes 786440 | tf_op jit(solution)/shard_map/ppermute | solution.py:58
  245.1 32.6 %collective-permute-start.39 = (f32[4,128,128]{2,1,0:T(8,128)S(1)}, f32[4,128,128]{2,1,0:T(8,128)S(1)}, u32[]{:S(2)}, u32[]{:S(2)}) collective-permute-start(f32[4,128,128]{2,1,0:T(8,128)S(1)} %add.397), channel_id=1, source_target_pairs={{0,37},{1,38},{2,39},{3,32},{4,33},{5,34},{6,35},{7,36},{8,45},{9,... | collective-permute-start | bytes 786440 | tf_op jit(solution)/shard_map/ppermute | solution.py:58
  247.4 32.4 %collective-permute-start.40 = (f32[4,128,128]{2,1,0:T(8,128)S(1)}, f32[4,128,128]{2,1,0:T(8,128)S(1)}, u32[]{:S(2)}, u32[]{:S(2)}) collective-permute-start(f32[4,128,128]{2,1,0:T(8,128)S(1)} %add.397), channel_id=1, source_target_pairs={{0,38},{1,39},{2,32},{3,33},{4,34},{5,35},{6,36},{7,37},{8,46},{9,... | collective-permute-start | bytes 786440 | tf_op jit(solution)/shard_map/ppermute | solution.py:58
  311.4 35.9 %collective-permute-start.42 = (f32[4,128,128]{2,1,0:T(8,128)S(1)}, f32[4,128,128]{2,1,0:T(8,128)S(1)}, u32[]{:S(2)}, u32[]{:S(2)}) collective-permute-start(f32[4,128,128]{2,1,0:T(8,128)S(1)} %add.398), channel_id=1, source_target_pairs={{0,64},{1,65},{2,66},{3,67},{4,68},{5,69},{6,70},{7,71},{8,72},{9,... | collective-permute-start | bytes 786440 | tf_op jit(solution)/shard_map/ppermute | solution.py:58
  316.0 43.4 %collective-permute-start.43 = (f32[4,128,128]{2,1,0:T(8,128)S(1)}, f32[4,128,128]{2,1,0:T(8,128)S(1)}, u32[]{:S(2)}, u32[]{:S(2)}) collective-permute-start(f32[4,128,128]{2,1,0:T(8,128)S(1)} %add.398), channel_id=1, source_target_pairs={{0,65},{1,66},{2,67},{3,68},{4,69},{5,70},{6,71},{7,64},{8,73},{9,... | collective-permute-start | bytes 786440 | tf_op jit(solution)/shard_map/ppermute | solution.py:58
  322.3 49.0 %collective-permute-start.44 = (f32[4,128,128]{2,1,0:T(8,128)S(1)}, f32[4,128,128]{2,1,0:T(8,128)S(1)}, u32[]{:S(2)}, u32[]{:S(2)}) collective-permute-start(f32[4,128,128]{2,1,0:T(8,128)S(1)} %add.398), channel_id=1, source_target_pairs={{0,66},{1,67},{2,68},{3,69},{4,70},{5,71},{6,64},{7,65},{8,74},{9,... | collective-permute-start | bytes 786440 | tf_op jit(solution)/shard_map/ppermute | solution.py:58
  325.7 57.6 %collective-permute-start.45 = (f32[4,128,128]{2,1,0:T(8,128)S(1)}, f32[4,128,128]{2,1,0:T(8,128)S(1)}, u32[]{:S(2)}, u32[]{:S(2)}) collective-permute-start(f32[4,128,128]{2,1,0:T(8,128)S(1)} %add.398), channel_id=1, source_target_pairs={{0,67},{1,68},{2,69},{3,70},{4,71},{5,64},{6,65},{7,66},{8,75},{9,... | collective-permute-start | bytes 786440 | tf_op jit(solution)/shard_map/ppermute | solution.py:58
  335.4 48.0 %collective-permute-start.46 = (f32[4,128,128]{2,1,0:T(8,128)S(1)}, f32[4,128,128]{2,1,0:T(8,128)S(1)}, u32[]{:S(2)}, u32[]{:S(2)}) collective-permute-start(f32[4,128,128]{2,1,0:T(8,128)S(1)} %add.398), channel_id=1, source_target_pairs={{0,68},{1,69},{2,70},{3,71},{4,64},{5,65},{6,66},{7,67},{8,76},{9,... | collective-permute-start | bytes 786440 | tf_op jit(solution)/shard_map/ppermute | solution.py:58
  347.2 38.4 %collective-permute-start.47 = (f32[4,128,128]{2,1,0:T(8,128)S(1)}, f32[4,128,128]{2,1,0:T(8,128)S(1)}, u32[]{:S(2)}, u32[]{:S(2)}) collective-permute-start(f32[4,128,128]{2,1,0:T(8,128)S(1)} %add.398), channel_id=1, source_target_pairs={{0,69},{1,70},{2,71},{3,64},{4,65},{5,66},{6,67},{7,68},{8,77},{9,... | collective-permute-start | bytes 786440 | tf_op jit(solution)/shard_map/ppermute | solution.py:58
  359.4 49.2 %collective-permute-start.48 = (f32[4,128,128]{2,1,0:T(8,128)S(1)}, f32[4,128,128]{2,1,0:T(8,128)S(1)}, u32[]{:S(2)}, u32[]{:S(2)}) collective-permute-start(f32[4,128,128]{2,1,0:T(8,128)S(1)} %add.398), channel_id=1, source_target_pairs={{0,70},{1,71},{2,64},{3,65},{4,66},{5,67},{6,68},{7,69},{8,78},{9,... | collective-permute-start | bytes 786440 | tf_op jit(solution)/shard_map/ppermute | solution.py:58
  371.4 40.5 %collective-permute-start.49 = (f32[4,128,128]{2,1,0:T(8,128)S(1)}, f32[4,128,128]{2,1,0:T(8,128)S(1)}, u32[]{:S(2)}, u32[]{:S(2)}) collective-permute-start(f32[4,128,128]{2,1,0:T(8,128)S(1)} %add.398), channel_id=1, source_target_pairs={{0,71},{1,64},{2,65},{3,66},{4,67},{5,68},{6,69},{7,70},{8,79},{9,... | collective-permute-start | bytes 786440 | tf_op jit(solution)/shard_map/ppermute | solution.py:58
  467.5 55.8 %collective-permute-start.50 = (f32[4,128,128]{2,1,0:T(8,128)S(1)}, f32[4,128,128]{2,1,0:T(8,128)S(1)}, u32[]{:S(2)}, u32[]{:S(2)}) collective-permute-start(f32[4,128,128]{2,1,0:T(8,128)S(1)} %add.399), channel_id=1, source_target_pairs={{0,128},{1,129},{2,130},{3,131},{4,132},{5,133},{6,134},{7,135},{8... | collective-permute-start | bytes 786440 | tf_op jit(solution)/shard_map/ppermute | solution.py:58
  475.9 59.3 %collective-permute-start.51 = (f32[4,128,128]{2,1,0:T(8,128)S(1)}, f32[4,128,128]{2,1,0:T(8,128)S(1)}, u32[]{:S(2)}, u32[]{:S(2)}) collective-permute-start(f32[4,128,128]{2,1,0:T(8,128)S(1)} %add.399), channel_id=1, source_target_pairs={{0,129},{1,130},{2,131},{3,132},{4,133},{5,134},{6,135},{7,128},{8... | collective-permute-start | bytes 786440 | tf_op jit(solution)/shard_map/ppermute | solution.py:58
  487.8 59.4 %collective-permute-start.52 = (f32[4,128,128]{2,1,0:T(8,128)S(1)}, f32[4,128,128]{2,1,0:T(8,128)S(1)}, u32[]{:S(2)}, u32[]{:S(2)}) collective-permute-start(f32[4,128,128]{2,1,0:T(8,128)S(1)} %add.399), channel_id=1, source_target_pairs={{0,130},{1,131},{2,132},{3,133},{4,134},{5,135},{6,128},{7,129},{8... | collective-permute-start | bytes 786440 | tf_op jit(solution)/shard_map/ppermute | solution.py:58
  499.6 59.5 %collective-permute-start.53 = (f32[4,128,128]{2,1,0:T(8,128)S(1)}, f32[4,128,128]{2,1,0:T(8,128)S(1)}, u32[]{:S(2)}, u32[]{:S(2)}) collective-permute-start(f32[4,128,128]{2,1,0:T(8,128)S(1)} %add.399), channel_id=1, source_target_pairs={{0,131},{1,132},{2,133},{3,134},{4,135},{5,128},{6,129},{7,130},{8... | collective-permute-start | bytes 786440 | tf_op jit(solution)/shard_map/ppermute | solution.py:58
  511.5 47.7 %collective-permute-start.54 = (f32[4,128,128]{2,1,0:T(8,128)S(1)}, f32[4,128,128]{2,1,0:T(8,128)S(1)}, u32[]{:S(2)}, u32[]{:S(2)}) collective-permute-start(f32[4,128,128]{2,1,0:T(8,128)S(1)} %add.399), channel_id=1, source_target_pairs={{0,132},{1,133},{2,134},{3,135},{4,128},{5,129},{6,130},{7,131},{8... | collective-permute-start | bytes 786440 | tf_op jit(solution)/shard_map/ppermute | solution.py:58
  523.3 35.9 %collective-permute-start.55 = (f32[4,128,128]{2,1,0:T(8,128)S(1)}, f32[4,128,128]{2,1,0:T(8,128)S(1)}, u32[]{:S(2)}, u32[]{:S(2)}) collective-permute-start(f32[4,128,128]{2,1,0:T(8,128)S(1)} %add.399), channel_id=1, source_target_pairs={{0,133},{1,134},{2,135},{3,128},{4,129},{5,130},{6,131},{7,132},{8... | collective-permute-start | bytes 786440 | tf_op jit(solution)/shard_map/ppermute | solution.py:58
  535.2 28.4 %collective-permute-start.56 = (f32[4,128,128]{2,1,0:T(8,128)S(1)}, f32[4,128,128]{2,1,0:T(8,128)S(1)}, u32[]{:S(2)}, u32[]{:S(2)}) collective-permute-start(f32[4,128,128]{2,1,0:T(8,128)S(1)} %add.399), channel_id=1, source_target_pairs={{0,134},{1,135},{2,128},{3,129},{4,130},{5,131},{6,132},{7,133},{8... | collective-permute-start | bytes 786440 | tf_op jit(solution)/shard_map/ppermute | solution.py:58
  547.1 36.5 %collective-permute-start.57 = (f32[4,128,128]{2,1,0:T(8,128)S(1)}, f32[4,128,128]{2,1,0:T(8,128)S(1)}, u32[]{:S(2)}, u32[]{:S(2)}) collective-permute-start(f32[4,128,128]{2,1,0:T(8,128)S(1)} %add.399), channel_id=1, source_target_pairs={{0,135},{1,128},{2,129},{3,130},{4,131},{5,132},{6,133},{7,134},{8... | collective-permute-start | bytes 786440 | tf_op jit(solution)/shard_map/ppermute | solution.py:58
  (37 other events, 526.7 us)

commit v3 on v2

--- a/solution.py
+++ b/solution.py
@@ -44,18 +44,11 @@
 
 
 def column_slabs(slab, lag):
-    n_tm = lax.axis_size("tm")
-    n_sp = lax.axis_size("space")
-    slots = []
-    for t in range(n_sp):
-        if t == 0 and lag == 0:
-            slots.append(slab)
-            continue
-        pairs = []
-        for k in range(n_tm):
-            for q in range(n_sp):
-                pairs.append((k * n_sp + q, ((k + lag) % n_tm) * n_sp + (q + t) % n_sp))
-        slots.append(lax.ppermute(slab, ("tm", "space"), pairs))
+    if lag:
+        slab = shifted(slab, "tm", lag)
+    slots = [slab]
+    for t in range(1, lax.axis_size("space")):
+        slots.append(shifted(slab, "space", t))
     return jnp.stack(slots, axis=0)
 
 
@@ -94,8 +87,8 @@
         return carry
 
     def one(i, carry):
-        lax.fori_loop(0, planes, first, 0)
-        lax.fori_loop(0, planes, second, 0)
+        lax.fori_loop(0, planes, first, 0, unroll=True)
+        lax.fori_loop(0, planes, second, 0, unroll=True)
         return carry
 
     lax.fori_loop(0, power, one, 0)

time: 746 us -> 478 us (0.64)
  starting transfers between devices: 278 us -> 120 us
  Pallas kernels: 217 us -> 78.1 us
  waiting for transfers between devices: 209 us -> 240 us
    ppermute x47 -> x0, starting transfers between devices: 225 us -> none  [column_slabs(): slots.append(lax.ppermute(slab, ('tm', 'space'), pairs))]
    ppermute x1 -> x48, waiting for transfers between devices: 6.45 us -> 175 us  [shifted(): return lax.ppermute(value, axis, pairs)]
    ppermute x47 -> x0, waiting for transfers between devices: 141 us -> none  [column_slabs(): slots.append(lax.ppermute(slab, ('tm', 'space'), pairs))]
    pallas_call x5, Pallas kernels: 217 us -> 78.1 us  [coarse_power(): pl.pallas_call(coarse_kernel, out_shape=jax.ShapeDtypeStruct((depth, rows...]
    ppermute x1 -> x48, starting transfers between devices: 0.08 us -> 64.5 us  [shifted(): return lax.ppermute(value, axis, pairs)]
  transfers between devices with their start and end apart: 64 -> 64, of which waited for: 39 -> 48; matrix products, arithmetic and copies ran while one was open for 3% -> 5% of each run, Pallas kernels for 0% -> 0%
where the time goes in v3:
time: 478 us; the launch traced here: 469 us
  waiting for transfers between devices  240 us (50%)
  starting transfers between devices  120 us (25%)
  Pallas kernels  78.1 us (16%)
  local copies, waits for them, and re-layouts  18.4 us (4%)
  other arithmetic  11.6 us (2%)
    ppermute x48, waiting for transfers between devices, shifted(): return lax.ppermute(value, axis, pairs)  175 us
    pallas_call x5, Pallas kernels, coarse_power(): pl.pallas_call(coarse_kernel, out_shape=jax.ShapeDtypeStruct((depth, rows...  78.1 us
    ppermute x48, starting transfers between devices, shifted(): return lax.ppermute(value, axis, pairs)  64.5 us
    ppermute x8, waiting for transfers between devices, extended(): lax.ppermute(lax.slice_in_dim(block, 0, width, axis=dim), axis, backward)  45.3 us
    ppermute x8, starting transfers between devices, extended(): lax.ppermute(lax.slice_in_dim(block, block.shape[dim] - width, None, axis...  30.6 us
    ppermute x8, starting transfers between devices, extended(): lax.ppermute(lax.slice_in_dim(block, 0, width, axis=dim), axis, backward)  25.2 us
    ppermute x8, waiting for transfers between devices, extended(): lax.ppermute(lax.slice_in_dim(block, block.shape[dim] - width, None, axis...  19.6 us
  transfers between devices with their start and end apart: 64, of which 48 were waited for; matrix products, arithmetic and copies ran while one was open for 5% of the time, Pallas kernels for 0%

profile of v3, /device:TPU:24, one launch (start us, length us, event | category | flops | bytes accessed | tf_op | source)
XLA Modules:
  0.0 469.3 jit_solution(202054670831193325)
XLA Ops:
  6.3 5.1 %collective-permute-start = (f32[2,128,128]{2,1,0:T(8,128)S(1)}, f32[2,128,128]{2,1,0:T(8,128)S(1)}, u32[]{:S(2)}, u32[]{:S(2)}) collective-permute-start(f32[2,128,128]{2,1,0:T(8,128)S(1)} %get-tuple-element.137), channel_id=1, source_target_pairs={{0,1},{1,2},{2,3},{3,4},{4,5},{5,6},{6,7},{8,9},{9,10},{10,11},{11... | collective-permute-start | bytes 393224 | tf_op jit(solution)/shard_map/ppermute | solution.py:21
  16.3 10.3 %collective-permute-done = f32[2,128,128]{2,1,0:T(8,128)S(1)} collective-permute-done((f32[2,128,128]{2,1,0:T(8,128)S(1)}, f32[2,128,128]{2,1,0:T(8,128)S(1)}, u32[]{:S(2)}, u32[]{:S(2)}) %collective-permute-start) | collective-permute-done | bytes 131104 | tf_op jit(solution)/shard_map/ppermute | solution.py:21
  26.7 8.0 %collective-permute-start.2 = (f32[5,1,128,128]{3,2,1,0:T(8,128)S(1)}, f32[5,1,128,128]{3,2,1,0:T(8,128)S(1)}, u32[]{:S(2)}, u32[]{:S(2)}) collective-permute-start(f32[5,1,128,128]{3,2,1,0:T(8,128)S(1)} %get-tuple-element.23), channel_id=1, source_target_pairs={{0,1},{1,2},{2,3},{3,4},{4,5},{5,6},{6,7},{8,9},{9,10},{10,11},{11... | collective-permute-start | bytes 983048 | tf_op jit(solution)/shard_map/ppermute | solution.py:21
  37.2 5.1 %collective-permute-done.2 = f32[5,1,128,128]{3,2,1,0:T(8,128)S(1)} collective-permute-done((f32[5,1,128,128]{3,2,1,0:T(8,128)S(1)}, f32[5,1,128,128]{3,2,1,0:T(8,128)S(1)}, u32[]{:S(2)}, u32[]{:S(2)}) %collective-permute-start.2) | collective-permute-done | bytes 327712 | tf_op jit(solution)/shard_map/ppermute | solution.py:21
  42.3 8.5 %collective-permute-done.3 = f32[5,1,128,128]{3,2,1,0:T(8,128)S(1)} collective-permute-done((f32[5,1,128,128]{3,2,1,0:T(8,128)S(1)}, f32[5,1,128,128]{3,2,1,0:T(8,128)S(1)}, u32[]{:S(2)}, u32[]{:S(2)}) %collective-permute-start.3) | collective-permute-done | bytes 327712 | tf_op jit(solution)/shard_map/ppermute | solution.py:24
  73.9 6.7 %collective-permute-done.7 = f32[2,128,128]{2,1,0:T(8,128)S(1)} collective-permute-done((f32[2,128,128]{2,1,0:T(8,128)S(1)}, f32[2,128,128]{2,1,0:T(8,128)S(1)}, u32[]{:S(2)}, u32[]{:S(2)}) %collective-permute-start.7) | collective-permute-done | bytes 131104 | tf_op jit(solution)/shard_map/ppermute | solution.py:24
  83.6 6.4 %collective-permute-done.8 = f32[4,128,128]{2,1,0:T(8,128)S(1)} collective-permute-done((f32[4,128,128]{2,1,0:T(8,128)S(1)}, f32[4,128,128]{2,1,0:T(8,128)S(1)}, u32[]{:S(2)}, u32[]{:S(2)}) %collective-permute-start.8) | collective-permute-done | bytes 262176 | tf_op jit(solution)/shard_map/ppermute | solution.py:32
  90.1 7.5 %collective-permute-start.9 = (f32[2,128,128]{2,1,0:T(8,128)S(1)}, f32[2,128,128]{2,1,0:T(8,128)S(1)}, u32[]{:S(2)}, u32[]{:S(2)}) collective-permute-start(f32[2,128,128]{2,1,0:T(8,128)S(1)} %get-tuple-element.132), channel_id=1, source_target_pairs={{0,1},{1,2},{2,3},{3,4},{4,5},{5,6},{6,7},{8,9},{9,10},{10,11},{11... | collective-permute-start | bytes 393224 | tf_op jit(solution)/shard_map/ppermute | solution.py:21
  100.5 8.3 %collective-permute-done.10 = f32[2,128,128]{2,1,0:T(8,128)S(1)} collective-permute-done((f32[2,128,128]{2,1,0:T(8,128)S(1)}, f32[2,128,128]{2,1,0:T(8,128)S(1)}, u32[]{:S(2)}, u32[]{:S(2)}) %collective-permute-start.10) | collective-permute-done | bytes 131104 | tf_op jit(solution)/shard_map/ppermute | solution.py:24
  141.1 10.9 %collective-permute-done.17 = f32[4,128,128]{2,1,0:T(8,128)S(1)} collective-permute-done((f32[4,128,128]{2,1,0:T(8,128)S(1)}, f32[4,128,128]{2,1,0:T(8,128)S(1)}, u32[]{:S(2)}, u32[]{:S(2)}) %collective-permute-start.17) | collective-permute-done | bytes 262176 | tf_op jit(solution)/shard_map/ppermute | solution.py:32
  161.2 6.5 %collective-permute-done.26 = f32[4,128,128]{2,1,0:T(8,128)S(1)} collective-permute-done((f32[4,128,128]{2,1,0:T(8,128)S(1)}, f32[4,128,128]{2,1,0:T(8,128)S(1)}, u32[]{:S(2)}, u32[]{:S(2)}) %collective-permute-start.26) | collective-permute-done | bytes 262176 | tf_op jit(solution)/shard_map/ppermute | solution.py:32
  173.3 6.8 %collective-permute-done.27 = f32[4,128,128]{2,1,0:T(8,128)S(1)} collective-permute-done((f32[4,128,128]{2,1,0:T(8,128)S(1)}, f32[4,128,128]{2,1,0:T(8,128)S(1)}, u32[]{:S(2)}, u32[]{:S(2)}) %collective-permute-start.27) | collective-permute-done | bytes 262176 | tf_op jit(solution)/shard_map/ppermute | solution.py:32
  180.1 5.2 %collective-permute-done.28 = f32[4,128,128]{2,1,0:T(8,128)S(1)} collective-permute-done((f32[4,128,128]{2,1,0:T(8,128)S(1)}, f32[4,128,128]{2,1,0:T(8,128)S(1)}, u32[]{:S(2)}, u32[]{:S(2)}) %collective-permute-start.28) | collective-permute-done | bytes 262176 | tf_op jit(solution)/shard_map/ppermute | solution.py:32
  185.3 5.9 %collective-permute-done.29 = f32[4,128,128]{2,1,0:T(8,128)S(1)} collective-permute-done((f32[4,128,128]{2,1,0:T(8,128)S(1)}, f32[4,128,128]{2,1,0:T(8,128)S(1)}, u32[]{:S(2)}, u32[]{:S(2)}) %collective-permute-start.29) | collective-permute-done | bytes 262176 | tf_op jit(solution)/shard_map/ppermute | solution.py:32
  196.1 6.8 %collective-permute-done.32 = f32[4,128,128]{2,1,0:T(8,128)S(1)} collective-permute-done((f32[4,128,128]{2,1,0:T(8,128)S(1)}, f32[4,128,128]{2,1,0:T(8,128)S(1)}, u32[]{:S(2)}, u32[]{:S(2)}) %collective-permute-start.32) | collective-permute-done | bytes 262176 | tf_op jit(solution)/shard_map/ppermute | solution.py:32
  203.0 6.3 %shard_map.38 = f32[4,128,128]{2,1,0:T(8,128)S(1)} custom-call(s32[2]{0:T(128)S(1)} %pad_add_fusion.1.place_ref, f32[8,4,128,128]{3,2,1,0:T(8,128)S(1)} %bitcast_dynamic-update-slice_fusion.24.slots_ref, f32[32,128,128]{2,1,0:T(8,128)S(1)} %get-tuple-element.20.w_ref, f32[32,128,128]{2,1,0:T(8,128)} %get-tuple-element.19.s_ref), custom_call_target="tpu_custom_call" | custom-call | flops 25165824 | bytes 6291456 | tf_op jit(solution)/shard_map/pallas_call | solution.py:103
  212.1 9.1 %collective-permute-done.34 = f32[4,128,128]{2,1,0:T(8,128)S(1)} collective-permute-done((f32[4,128,128]{2,1,0:T(8,128)S(1)}, f32[4,128,128]{2,1,0:T(8,128)S(1)}, u32[]{:S(2)}, u32[]{:S(2)}) %collective-permute-start.34) | collective-permute-done | bytes 262176 | tf_op jit(solution)/shard_map/ppermute | solution.py:32
  221.2 5.3 %collective-permute-start.36 = (f32[4,128,128]{2,1,0:T(8,128)S(1)}, f32[4,128,128]{2,1,0:T(8,128)S(1)}, u32[]{:S(2)}, u32[]{:S(2)}) collective-permute-start(f32[4,128,128]{2,1,0:T(8,128)S(1)} %collective-permute-done.34), channel_id=1, source_target_pairs={{0,2},{1,3},{2,4},{3,5},{4,6},{5,7},{6,0},{7,1},{8,10},{9,11},{10,... | collective-permute-start | bytes 786440 | tf_op jit(solution)/shard_map/ppermute | solution.py:32
  235.2 5.5 %collective-permute-done.37 = f32[4,128,128]{2,1,0:T(8,128)S(1)} collective-permute-done((f32[4,128,128]{2,1,0:T(8,128)S(1)}, f32[4,128,128]{2,1,0:T(8,128)S(1)}, u32[]{:S(2)}, u32[]{:S(2)}) %collective-permute-start.37) | collective-permute-done | bytes 262176 | tf_op jit(solution)/shard_map/ppermute | solution.py:32
  254.8 10.7 %shard_map.39 = f32[4,128,128]{2,1,0:T(8,128)S(1)} custom-call(s32[2]{0:T(128)S(1)} %pad_add_fusion.2.place_ref, f32[8,4,128,128]{3,2,1,0:T(8,128)S(1)} %bitcast_dynamic-update-slice_fusion.16.slots_ref, f32[32,128,128]{2,1,0:T(8,128)S(1)} %get-tuple-element.20.w_ref, f32[32,128,128]{2,1,0:T(8,128)} %get-tuple-element.19.s_ref), custom_call_target="tpu_custom_call" | custom-call | flops 50331648 | bytes 6291456 | tf_op jit(solution)/shard_map/pallas_call | solution.py:103
  265.6 13.8 %collective-permute-done.42 = f32[4,128,128]{2,1,0:T(8,128)S(1)} collective-permute-done((f32[4,128,128]{2,1,0:T(8,128)S(1)}, f32[4,128,128]{2,1,0:T(8,128)S(1)}, u32[]{:S(2)}, u32[]{:S(2)}) %collective-permute-start.42) | collective-permute-done | bytes 262176 | tf_op jit(solution)/shard_map/ppermute | solution.py:32
  279.5 6.5 %collective-permute-start.44 = (f32[4,128,128]{2,1,0:T(8,128)S(1)}, f32[4,128,128]{2,1,0:T(8,128)S(1)}, u32[]{:S(2)}, u32[]{:S(2)}) collective-permute-start(f32[4,128,128]{2,1,0:T(8,128)S(1)} %collective-permute-done.42), channel_id=1, source_target_pairs={{0,2},{1,3},{2,4},{3,5},{4,6},{5,7},{6,0},{7,1},{8,10},{9,11},{10,... | collective-permute-start | bytes 786440 | tf_op jit(solution)/shard_map/ppermute | solution.py:32
  302.2 9.8 %collective-permute-done.46 = f32[4,128,128]{2,1,0:T(8,128)S(1)} collective-permute-done((f32[4,128,128]{2,1,0:T(8,128)S(1)}, f32[4,128,128]{2,1,0:T(8,128)S(1)}, u32[]{:S(2)}, u32[]{:S(2)}) %collective-permute-start.46) | collective-permute-done | bytes 262176 | tf_op jit(solution)/shard_map/ppermute | solution.py:32
  316.5 19.6 %shard_map.40 = f32[4,128,128]{2,1,0:T(8,128)S(1)} custom-call(s32[2]{0:T(128)S(1)} %pad_add_fusion.3.place_ref, f32[8,4,128,128]{3,2,1,0:T(8,128)S(1)} %bitcast_dynamic-update-slice_fusion.8.slots_ref, f32[32,128,128]{2,1,0:T(8,128)S(1)} %get-tuple-element.20.w_ref, f32[32,128,128]{2,1,0:T(8,128)} %get-tuple-element.19.s_ref), custom_call_target="tpu_custom_call" | custom-call | flops 100663296 | bytes 6291456 | tf_op jit(solution)/shard_map/pallas_call | solution.py:103
  339.0 12.1 %collective-permute-done.50 = f32[4,128,128]{2,1,0:T(8,128)S(1)} collective-permute-done((f32[4,128,128]{2,1,0:T(8,128)S(1)}, f32[4,128,128]{2,1,0:T(8,128)S(1)}, u32[]{:S(2)}, u32[]{:S(2)}) %collective-permute-start.50) | collective-permute-done | bytes 262176 | tf_op jit(solution)/shard_map/ppermute | solution.py:32
  351.4 6.0 %collective-permute-start.52 = (f32[4,128,128]{2,1,0:T(8,128)S(1)}, f32[4,128,128]{2,1,0:T(8,128)S(1)}, u32[]{:S(2)}, u32[]{:S(2)}) collective-permute-start(f32[4,128,128]{2,1,0:T(8,128)S(1)} %collective-permute-done.50), channel_id=1, source_target_pairs={{0,2},{1,3},{2,4},{3,5},{4,6},{5,7},{6,0},{7,1},{8,10},{9,11},{10,... | collective-permute-start | bytes 786440 | tf_op jit(solution)/shard_map/ppermute | solution.py:32
  360.7 5.1 %collective-permute-done.51 = f32[4,128,128]{2,1,0:T(8,128)S(1)} collective-permute-done((f32[4,128,128]{2,1,0:T(8,128)S(1)}, f32[4,128,128]{2,1,0:T(8,128)S(1)}, u32[]{:S(2)}, u32[]{:S(2)}) %collective-permute-start.51) | collective-permute-done | bytes 262176 | tf_op jit(solution)/shard_map/ppermute | solution.py:32
  369.1 6.5 %collective-permute-done.53 = f32[4,128,128]{2,1,0:T(8,128)S(1)} collective-permute-done((f32[4,128,128]{2,1,0:T(8,128)S(1)}, f32[4,128,128]{2,1,0:T(8,128)S(1)}, u32[]{:S(2)}, u32[]{:S(2)}) %collective-permute-start.53) | collective-permute-done | bytes 262176 | tf_op jit(solution)/shard_map/ppermute | solution.py:32
  388.3 37.5 %shard_map.41 = f32[4,128,128]{2,1,0:T(8,128)S(1)} custom-call(s32[2]{0:T(128)S(1)} %pad_add_fusion.4.place_ref, f32[8,4,128,128]{3,2,1,0:T(8,128)S(1)} %bitcast_dynamic-update-slice_fusion.slots_ref, f32[32,128,128]{2,1,0:T(8,128)S(1)} %get-tuple-element.20.w_ref, f32[32,128,128]{2,1,0:T(8,128)} %get-tuple-element.19.s_ref), custom_call_target="tpu_custom_call" | custom-call | flops 201326592 | bytes 6291456 | tf_op jit(solution)/shard_map/pallas_call | solution.py:103
  432.7 5.5 %collective-permute-done.59 = f32[2,128,128]{2,1,0:T(8,128)S(1)} collective-permute-done((f32[2,128,128]{2,1,0:T(8,128)S(1)}, f32[2,128,128]{2,1,0:T(8,128)S(1)}, u32[]{:S(2)}, u32[]{:S(2)}) %collective-permute-start.59) | collective-permute-done | bytes 131104 | tf_op jit(solution)/shard_map/ppermute | solution.py:24
  446.6 5.9 %collective-permute-done.61 = f32[2,128,128]{2,1,0:T(8,128)S(1)} collective-permute-done((f32[2,128,128]{2,1,0:T(8,128)S(1)}, f32[2,128,128]{2,1,0:T(8,128)S(1)}, u32[]{:S(2)}, u32[]{:S(2)}) %collective-permute-start.61) | collective-permute-done | bytes 131104 | tf_op jit(solution)/shard_map/ppermute | solution.py:24
  460.9 5.5 %collective-permute-done.63 = f32[2,128,128]{2,1,0:T(8,128)S(1)} collective-permute-done((f32[2,128,128]{2,1,0:T(8,128)S(1)}, f32[2,128,128]{2,1,0:T(8,128)S(1)}, u32[]{:S(2)}, u32[]{:S(2)}) %collective-permute-start.63) | collective-permute-done | bytes 131104 | tf_op jit(solution)/shard_map/ppermute | solution.py:24
  (256 shorter events, 189.1 us)
Async XLA Ops:
  0.0 54.1 %collective-permute-start.19 = (f32[4,128,128]{2,1,0:T(8,128)}, f32[4,128,128]{2,1,0:T(8,128)}, u32[]{:S(2)}, u32[]{:S(2)}) collective-permute-start(f32[4,128,128]{2,1,0:T(8,128)} %param.4), channel_id=1, source_target_pairs={{0,1},{1,2},{2,3},{3,4},{4,5},{5,6},{6,7},{7,0},{8,9},{9,10},{10,1... | collective-permute-start | bytes 786440 | tf_op jit(solution)/shard_map/ppermute | solution.py:32
  2.7 65.4 %collective-permute-start.20 = (f32[4,128,128]{2,1,0:T(8,128)}, f32[4,128,128]{2,1,0:T(8,128)S(1)}, u32[]{:S(2)}, u32[]{:S(2)}) collective-permute-start(f32[4,128,128]{2,1,0:T(8,128)} %param.4), channel_id=1, source_target_pairs={{0,2},{1,3},{2,4},{3,5},{4,6},{5,7},{6,0},{7,1},{8,10},{9,11},{10,... | collective-permute-start | bytes 786440 | tf_op jit(solution)/shard_map/ppermute | solution.py:32
  5.3 76.8 %collective-permute-start.21 = (f32[4,128,128]{2,1,0:T(8,128)}, f32[4,128,128]{2,1,0:T(8,128)S(1)}, u32[]{:S(2)}, u32[]{:S(2)}) collective-permute-start(f32[4,128,128]{2,1,0:T(8,128)} %param.4), channel_id=1, source_target_pairs={{0,3},{1,4},{2,5},{3,6},{4,7},{5,0},{6,1},{7,2},{8,11},{9,12},{10,... | collective-permute-start | bytes 786440 | tf_op jit(solution)/shard_map/ppermute | solution.py:32
  6.3 20.4 %collective-permute-start = (f32[2,128,128]{2,1,0:T(8,128)S(1)}, f32[2,128,128]{2,1,0:T(8,128)S(1)}, u32[]{:S(2)}, u32[]{:S(2)}) collective-permute-start(f32[2,128,128]{2,1,0:T(8,128)S(1)} %get-tuple-element.137), channel_id=1, source_target_pairs={{0,1},{1,2},{2,3},{3,4},{4,5},{5,6},{6,7},{8,9},{9,10},{10,11},{11... | collective-permute-start | bytes 393224 | tf_op jit(solution)/shard_map/ppermute | solution.py:21
  11.4 23.4 %collective-permute-start.1 = (f32[2,128,128]{2,1,0:T(8,128)S(1)}, f32[2,128,128]{2,1,0:T(8,128)S(1)}, u32[]{:S(2)}, u32[]{:S(2)}) collective-permute-start(f32[2,128,128]{2,1,0:T(8,128)S(1)} %get-tuple-element.138), channel_id=1, source_target_pairs={{1,0},{2,1},{3,2},{4,3},{5,4},{6,5},{7,6},{9,8},{10,9},{11,10},{12... | collective-permute-start | bytes 393224 | tf_op jit(solution)/shard_map/ppermute | solution.py:24
  42.3 40.6 %collective-permute-start.22 = (f32[4,128,128]{2,1,0:T(8,128)S(1)}, f32[4,128,128]{2,1,0:T(8,128)S(1)}, u32[]{:S(2)}, u32[]{:S(2)}) collective-permute-start(f32[4,128,128]{2,1,0:T(8,128)S(1)} %copy-done.2), channel_id=1, source_target_pairs={{0,4},{1,5},{2,6},{3,7},{4,0},{5,1},{6,2},{7,3},{8,12},{9,13},{10,... | collective-permute-start | bytes 786440 | tf_op jit(solution)/shard_map/ppermute | solution.py:32
  59.7 38.0 %collective-permute-start.23 = (f32[4,128,128]{2,1,0:T(8,128)S(1)}, f32[4,128,128]{2,1,0:T(8,128)S(1)}, u32[]{:S(2)}, u32[]{:S(2)}) collective-permute-start(f32[4,128,128]{2,1,0:T(8,128)S(1)} %copy-done.2), channel_id=1, source_target_pairs={{0,5},{1,6},{2,7},{3,0},{4,1},{5,2},{6,3},{7,4},{8,13},{9,14},{10,... | collective-permute-start | bytes 786440 | tf_op jit(solution)/shard_map/ppermute | solution.py:32
  73.9 36.6 %collective-permute-start.24 = (f32[4,128,128]{2,1,0:T(8,128)S(1)}, f32[4,128,128]{2,1,0:T(8,128)S(1)}, u32[]{:S(2)}, u32[]{:S(2)}) collective-permute-start(f32[4,128,128]{2,1,0:T(8,128)S(1)} %copy-done.2), channel_id=1, source_target_pairs={{0,6},{1,7},{2,0},{3,1},{4,2},{5,3},{6,4},{7,5},{8,14},{9,15},{10,... | collective-permute-start | bytes 786440 | tf_op jit(solution)/shard_map/ppermute | solution.py:32
  80.5 30.6 %collective-permute-start.25 = (f32[4,128,128]{2,1,0:T(8,128)S(1)}, f32[4,128,128]{2,1,0:T(8,128)S(1)}, u32[]{:S(2)}, u32[]{:S(2)}) collective-permute-start(f32[4,128,128]{2,1,0:T(8,128)S(1)} %copy-done.2), channel_id=1, source_target_pairs={{0,7},{1,0},{2,1},{3,2},{4,3},{5,4},{6,5},{7,6},{8,15},{9,8},{10,9... | collective-permute-start | bytes 786440 | tf_op jit(solution)/shard_map/ppermute | solution.py:32
  126.9 25.2 %collective-permute-start.17 = (f32[4,128,128]{2,1,0:T(8,128)S(1)}, f32[4,128,128]{2,1,0:T(8,128)S(1)}, u32[]{:S(2)}, u32[]{:S(2)}) collective-permute-start(f32[4,128,128]{2,1,0:T(8,128)S(1)} %collective-permute-done.11), channel_id=1, source_target_pairs={{0,6},{1,7},{2,0},{3,1},{4,2},{5,3},{6,4},{7,5},{8,14},{9,15},{10,... | collective-permute-start | bytes 786440 | tf_op jit(solution)/shard_map/ppermute | solution.py:32
  135.4 16.7 %collective-permute-start.18 = (f32[4,128,128]{2,1,0:T(8,128)S(1)}, f32[4,128,128]{2,1,0:T(8,128)S(1)}, u32[]{:S(2)}, u32[]{:S(2)}) collective-permute-start(f32[4,128,128]{2,1,0:T(8,128)S(1)} %collective-permute-done.11), channel_id=1, source_target_pairs={{0,7},{1,0},{2,1},{3,2},{4,3},{5,4},{6,5},{7,6},{8,15},{9,8},{10,9... | collective-permute-start | bytes 786440 | tf_op jit(solution)/shard_map/ppermute | solution.py:32
  167.8 17.5 %collective-permute-start.28 = (f32[4,128,128]{2,1,0:T(8,128)S(1)}, f32[4,128,128]{2,1,0:T(8,128)S(1)}, u32[]{:S(2)}, u32[]{:S(2)}) collective-permute-start(f32[4,128,128]{2,1,0:T(8,128)S(1)} %collective-permute-done.26), channel_id=1, source_target_pairs={{0,2},{1,3},{2,4},{3,5},{4,6},{5,7},{6,0},{7,1},{8,10},{9,11},{10,... | collective-permute-start | bytes 786440 | tf_op jit(solution)/shard_map/ppermute | solution.py:32
  169.0 22.2 %collective-permute-start.29 = (f32[4,128,128]{2,1,0:T(8,128)S(1)}, f32[4,128,128]{2,1,0:T(8,128)S(1)}, u32[]{:S(2)}, u32[]{:S(2)}) collective-permute-start(f32[4,128,128]{2,1,0:T(8,128)S(1)} %collective-permute-done.26), channel_id=1, source_target_pairs={{0,3},{1,4},{2,5},{3,6},{4,7},{5,0},{6,1},{7,2},{8,11},{9,12},{10,... | collective-permute-start | bytes 786440 | tf_op jit(solution)/shard_map/ppermute | solution.py:32
  169.1 27.0 %collective-permute-start.30 = (f32[4,128,128]{2,1,0:T(8,128)S(1)}, f32[4,128,128]{2,1,0:T(8,128)S(1)}, u32[]{:S(2)}, u32[]{:S(2)}) collective-permute-start(f32[4,128,128]{2,1,0:T(8,128)S(1)} %collective-permute-done.26), channel_id=1, source_target_pairs={{0,4},{1,5},{2,6},{3,7},{4,0},{5,1},{6,2},{7,3},{8,12},{9,13},{10,... | collective-permute-start | bytes 786440 | tf_op jit(solution)/shard_map/ppermute | solution.py:32
  173.3 22.8 %collective-permute-start.31 = (f32[4,128,128]{2,1,0:T(8,128)S(1)}, f32[4,128,128]{2,1,0:T(8,128)S(1)}, u32[]{:S(2)}, u32[]{:S(2)}) collective-permute-start(f32[4,128,128]{2,1,0:T(8,128)S(1)} %collective-permute-done.26), channel_id=1, source_target_pairs={{0,5},{1,6},{2,7},{3,0},{4,1},{5,2},{6,3},{7,4},{8,13},{9,14},{10,... | collective-permute-start | bytes 786440 | tf_op jit(solution)/shard_map/ppermute | solution.py:32
  180.1 22.8 %collective-permute-start.32 = (f32[4,128,128]{2,1,0:T(8,128)S(1)}, f32[4,128,128]{2,1,0:T(8,128)S(1)}, u32[]{:S(2)}, u32[]{:S(2)}) collective-permute-start(f32[4,128,128]{2,1,0:T(8,128)S(1)} %collective-permute-done.26), channel_id=1, source_target_pairs={{0,6},{1,7},{2,0},{3,1},{4,2},{5,3},{6,4},{7,5},{8,14},{9,15},{10,... | collective-permute-start | bytes 786440 | tf_op jit(solution)/shard_map/ppermute | solution.py:32
  185.2 17.7 %collective-permute-start.33 = (f32[4,128,128]{2,1,0:T(8,128)S(1)}, f32[4,128,128]{2,1,0:T(8,128)S(1)}, u32[]{:S(2)}, u32[]{:S(2)}) collective-permute-start(f32[4,128,128]{2,1,0:T(8,128)S(1)} %collective-permute-done.26), channel_id=1, source_target_pairs={{0,7},{1,0},{2,1},{3,2},{4,3},{5,4},{6,5},{7,6},{8,15},{9,8},{10,9... | collective-permute-start | bytes 786440 | tf_op jit(solution)/shard_map/ppermute | solution.py:32
  226.7 17.8 %collective-permute-start.38 = (f32[4,128,128]{2,1,0:T(8,128)S(1)}, f32[4,128,128]{2,1,0:T(8,128)S(1)}, u32[]{:S(2)}, u32[]{:S(2)}) collective-permute-start(f32[4,128,128]{2,1,0:T(8,128)S(1)} %collective-permute-done.34), channel_id=1, source_target_pairs={{0,4},{1,5},{2,6},{3,7},{4,0},{5,1},{6,2},{7,3},{8,12},{9,13},{10,... | collective-permute-start | bytes 786440 | tf_op jit(solution)/shard_map/ppermute | solution.py:32
  226.8 20.2 %collective-permute-start.39 = (f32[4,128,128]{2,1,0:T(8,128)S(1)}, f32[4,128,128]{2,1,0:T(8,128)S(1)}, u32[]{:S(2)}, u32[]{:S(2)}) collective-permute-start(f32[4,128,128]{2,1,0:T(8,128)S(1)} %collective-permute-done.34), channel_id=1, source_target_pairs={{0,5},{1,6},{2,7},{3,0},{4,1},{5,2},{6,3},{7,4},{8,13},{9,14},{10,... | collective-permute-start | bytes 786440 | tf_op jit(solution)/shard_map/ppermute | solution.py:32
  233.2 18.6 %collective-permute-start.40 = (f32[4,128,128]{2,1,0:T(8,128)S(1)}, f32[4,128,128]{2,1,0:T(8,128)S(1)}, u32[]{:S(2)}, u32[]{:S(2)}) collective-permute-start(f32[4,128,128]{2,1,0:T(8,128)S(1)} %collective-permute-done.34), channel_id=1, source_target_pairs={{0,6},{1,7},{2,0},{3,1},{4,2},{5,3},{6,4},{7,5},{8,14},{9,15},{10,... | collective-permute-start | bytes 786440 | tf_op jit(solution)/shard_map/ppermute | solution.py:32
  234.9 19.8 %collective-permute-start.41 = (f32[4,128,128]{2,1,0:T(8,128)S(1)}, f32[4,128,128]{2,1,0:T(8,128)S(1)}, u32[]{:S(2)}, u32[]{:S(2)}) collective-permute-start(f32[4,128,128]{2,1,0:T(8,128)S(1)} %collective-permute-done.34), channel_id=1, source_target_pairs={{0,7},{1,0},{2,1},{3,2},{4,3},{5,4},{6,5},{7,6},{8,15},{9,8},{10,9... | collective-permute-start | bytes 786440 | tf_op jit(solution)/shard_map/ppermute | solution.py:32
  279.5 16.4 %collective-permute-start.44 = (f32[4,128,128]{2,1,0:T(8,128)S(1)}, f32[4,128,128]{2,1,0:T(8,128)S(1)}, u32[]{:S(2)}, u32[]{:S(2)}) collective-permute-start(f32[4,128,128]{2,1,0:T(8,128)S(1)} %collective-permute-done.42), channel_id=1, source_target_pairs={{0,2},{1,3},{2,4},{3,5},{4,6},{5,7},{6,0},{7,1},{8,10},{9,11},{10,... | collective-permute-start | bytes 786440 | tf_op jit(solution)/shard_map/ppermute | solution.py:32
  286.0 26.0 %collective-permute-start.46 = (f32[4,128,128]{2,1,0:T(8,128)S(1)}, f32[4,128,128]{2,1,0:T(8,128)S(1)}, u32[]{:S(2)}, u32[]{:S(2)}) collective-permute-start(f32[4,128,128]{2,1,0:T(8,128)S(1)} %collective-permute-done.42), channel_id=1, source_target_pairs={{0,4},{1,5},{2,6},{3,7},{4,0},{5,1},{6,2},{7,3},{8,12},{9,13},{10,... | collective-permute-start | bytes 786440 | tf_op jit(solution)/shard_map/ppermute | solution.py:32
  286.1 26.3 %collective-permute-start.47 = (f32[4,128,128]{2,1,0:T(8,128)S(1)}, f32[4,128,128]{2,1,0:T(8,128)S(1)}, u32[]{:S(2)}, u32[]{:S(2)}) collective-permute-start(f32[4,128,128]{2,1,0:T(8,128)S(1)} %collective-permute-done.42), channel_id=1, source_target_pairs={{0,5},{1,6},{2,7},{3,0},{4,1},{5,2},{6,3},{7,4},{8,13},{9,14},{10,... | collective-permute-start | bytes 786440 | tf_op jit(solution)/shard_map/ppermute | solution.py:32
  289.3 23.5 %collective-permute-start.48 = (f32[4,128,128]{2,1,0:T(8,128)S(1)}, f32[4,128,128]{2,1,0:T(8,128)S(1)}, u32[]{:S(2)}, u32[]{:S(2)}) collective-permute-start(f32[4,128,128]{2,1,0:T(8,128)S(1)} %collective-permute-done.42), channel_id=1, source_target_pairs={{0,6},{1,7},{2,0},{3,1},{4,2},{5,3},{6,4},{7,5},{8,14},{9,15},{10,... | collective-permute-start | bytes 786440 | tf_op jit(solution)/shard_map/ppermute | solution.py:32
  295.9 20.6 %collective-permute-start.49 = (f32[4,128,128]{2,1,0:T(8,128)S(1)}, f32[4,128,128]{2,1,0:T(8,128)S(1)}, u32[]{:S(2)}, u32[]{:S(2)}) collective-permute-start(f32[4,128,128]{2,1,0:T(8,128)S(1)} %collective-permute-done.42), channel_id=1, source_target_pairs={{0,7},{1,0},{2,1},{3,2},{4,3},{5,4},{6,5},{7,6},{8,15},{9,8},{10,9... | collective-permute-start | bytes 786440 | tf_op jit(solution)/shard_map/ppermute | solution.py:32
  351.4 17.7 %collective-permute-start.52 = (f32[4,128,128]{2,1,0:T(8,128)S(1)}, f32[4,128,128]{2,1,0:T(8,128)S(1)}, u32[]{:S(2)}, u32[]{:S(2)}) collective-permute-start(f32[4,128,128]{2,1,0:T(8,128)S(1)} %collective-permute-done.50), channel_id=1, source_target_pairs={{0,2},{1,3},{2,4},{3,5},{4,6},{5,7},{6,0},{7,1},{8,10},{9,11},{10,... | collective-permute-start | bytes 786440 | tf_op jit(solution)/shard_map/ppermute | solution.py:32
  357.4 18.2 %collective-permute-start.53 = (f32[4,128,128]{2,1,0:T(8,128)S(1)}, f32[4,128,128]{2,1,0:T(8,128)S(1)}, u32[]{:S(2)}, u32[]{:S(2)}) collective-permute-start(f32[4,128,128]{2,1,0:T(8,128)S(1)} %collective-permute-done.50), channel_id=1, source_target_pairs={{0,3},{1,4},{2,5},{3,6},{4,7},{5,0},{6,1},{7,2},{8,11},{9,12},{10,... | collective-permute-start | bytes 786440 | tf_op jit(solution)/shard_map/ppermute | solution.py:32
  357.5 23.1 %collective-permute-start.54 = (f32[4,128,128]{2,1,0:T(8,128)S(1)}, f32[4,128,128]{2,1,0:T(8,128)S(1)}, u32[]{:S(2)}, u32[]{:S(2)}) collective-permute-start(f32[4,128,128]{2,1,0:T(8,128)S(1)} %collective-permute-done.50), channel_id=1, source_target_pairs={{0,4},{1,5},{2,6},{3,7},{4,0},{5,1},{6,2},{7,3},{8,12},{9,13},{10,... | collective-permute-start | bytes 786440 | tf_op jit(solution)/shard_map/ppermute | solution.py:32
  357.6 23.8 %collective-permute-start.55 = (f32[4,128,128]{2,1,0:T(8,128)S(1)}, f32[4,128,128]{2,1,0:T(8,128)S(1)}, u32[]{:S(2)}, u32[]{:S(2)}) collective-permute-start(f32[4,128,128]{2,1,0:T(8,128)S(1)} %collective-permute-done.50), channel_id=1, source_target_pairs={{0,5},{1,6},{2,7},{3,0},{4,1},{5,2},{6,3},{7,4},{8,13},{9,14},{10,... | collective-permute-start | bytes 786440 | tf_op jit(solution)/shard_map/ppermute | solution.py:32
  365.9 20.0 %collective-permute-start.56 = (f32[4,128,128]{2,1,0:T(8,128)S(1)}, f32[4,128,128]{2,1,0:T(8,128)S(1)}, u32[]{:S(2)}, u32[]{:S(2)}) collective-permute-start(f32[4,128,128]{2,1,0:T(8,128)S(1)} %collective-permute-done.50), channel_id=1, source_target_pairs={{0,6},{1,7},{2,0},{3,1},{4,2},{5,3},{6,4},{7,5},{8,14},{9,15},{10,... | collective-permute-start | bytes 786440 | tf_op jit(solution)/shard_map/ppermute | solution.py:32
  369.1 19.2 %collective-permute-start.57 = (f32[4,128,128]{2,1,0:T(8,128)S(1)}, f32[4,128,128]{2,1,0:T(8,128)S(1)}, u32[]{:S(2)}, u32[]{:S(2)}) collective-permute-start(f32[4,128,128]{2,1,0:T(8,128)S(1)} %collective-permute-done.50), channel_id=1, source_target_pairs={{0,7},{1,0},{2,1},{3,2},{4,3},{5,4},{6,5},{7,6},{8,15},{9,8},{10,9... | collective-permute-start | bytes 786440 | tf_op jit(solution)/shard_map/ppermute | solution.py:32
  (35 other events, 426.6 us)

commit v4 on v3

--- a/solution.py
+++ b/solution.py
@@ -133,10 +133,6 @@
     n_sp = lax.axis_size("space")
     me_sp = lax.axis_index("space")
     order = lax.rem(me_sp - jnp.arange(n_sp, dtype=jnp.int32) + n_sp, n_sp)
-    kappa_full = jnp.take(column_slabs(conductivity, 0), order, axis=0)
-    kappa_full = kappa_full.reshape((-1,) + conductivity.shape[1:])
-    coarse_weight = CF * step_length * kappa_full
-    coarse_scaled = 1.0 + 6.0 * coarse_weight
     place = me_sp.astype(jnp.int32)
 
     def advance(state, weight, scaled, source):
@@ -162,8 +158,15 @@
     defect = fine_step(before, 0) - anchor
 
     count = lax.axis_size("tm")
-    total = defect
-    lag = 1
+    depth = defect.shape[0]
+    moved = shifted(defect, "tm", 1)
+    slots = column_slabs(jnp.concatenate([moved, conductivity], axis=0), 0)
+    kappa_full = jnp.take(slots[:, depth:], order, axis=0)
+    kappa_full = kappa_full.reshape((-1,) + conductivity.shape[1:])
+    coarse_weight = CF * step_length * kappa_full
+    coarse_scaled = 1.0 + 6.0 * coarse_weight
+    total = defect + coarse_power(1, place, slots[:, :depth], coarse_weight, coarse_scaled)
+    lag = 2
     while lag < count:
         slots = column_slabs(total, lag)
         total = total + coarse_power(lag, place, slots, coarse_weight, coarse_scaled)

time: 478 us -> 489 us (1.023)
  starting transfers between devices: 120 us -> 154 us
  waiting for transfers between devices: 240 us -> 220 us
    ppermute x48 -> x41, starting transfers between devices: 64.5 us -> 103 us  [shifted(): return lax.ppermute(value, axis, pairs)]
    ppermute x8, waiting for transfers between devices: 19.6 us -> 9.95 us  [extended(): lax.ppermute(lax.slice_in_dim(block, block.shape[dim] - width, None, axis...]
    ppermute x8, starting transfers between devices: 30.6 us -> 23.6 us  [extended(): lax.ppermute(lax.slice_in_dim(block, block.shape[dim] - width, None, axis...]
    ppermute x48 -> x41, waiting for transfers between devices: 175 us -> 169 us  [shifted(): return lax.ppermute(value, axis, pairs)]
  transfers between devices with their start and end apart: 64 -> 57, of which waited for: 48 -> 49; matrix products, arithmetic and copies ran while one was open for 5% -> 1% of each run, Pallas kernels for 0% -> 0%
where the time goes in v4:
time: 489 us; the launch traced here: 481 us
  waiting for transfers between devices  220 us (45%)
  starting transfers between devices  154 us (31%)
  Pallas kernels  78.3 us (16%)
  local copies, waits for them, and re-layouts  14.8 us (3%)
  other arithmetic  11.7 us (2%)
    ppermute x41, waiting for transfers between devices, shifted(): return lax.ppermute(value, axis, pairs)  169 us
    ppermute x41, starting transfers between devices, shifted(): return lax.ppermute(value, axis, pairs)  103 us
    pallas_call x5, Pallas kernels, coarse_power(): pl.pallas_call(coarse_kernel, out_shape=jax.ShapeDtypeStruct((depth, rows...  78.3 us
    ppermute x8, waiting for transfers between devices, extended(): lax.ppermute(lax.slice_in_dim(block, 0, width, axis=dim), axis, backward)  40.9 us
    ppermute x8, starting transfers between devices, extended(): lax.ppermute(lax.slice_in_dim(block, 0, width, axis=dim), axis, backward)  27.4 us
    ppermute x8, starting transfers between devices, extended(): lax.ppermute(lax.slice_in_dim(block, block.shape[dim] - width, None, axis...  23.6 us
    ppermute x8, waiting for transfers between devices, extended(): lax.ppermute(lax.slice_in_dim(block, block.shape[dim] - width, None, axis...  9.95 us
  transfers between devices with their start and end apart: 57, of which 49 were waited for; matrix products, arithmetic and copies ran while one was open for 1% of the time, Pallas kernels for 0%

profile of v4, /device:TPU:24, one launch (start us, length us, event | category | flops | bytes accessed | tf_op | source)
XLA Modules:
  0.0 480.8 jit_solution(8600887652513161453)
XLA Ops:
  8.7 7.5 %collective-permute-start.2 = (f32[5,1,128,128]{3,2,1,0:T(8,128)S(1)}, f32[5,1,128,128]{3,2,1,0:T(8,128)S(1)}, u32[]{:S(2)}, u32[]{:S(2)}) collective-permute-start(f32[5,1,128,128]{3,2,1,0:T(8,128)S(1)} %get-tuple-element.25), channel_id=1, source_target_pairs={{0,1},{1,2},{2,3},{3,4},{4,5},{5,6},{6,7},{8,9},{9,10},{10,11},{11... | collective-permute-start | bytes 983048 | tf_op jit(solution)/shard_map/ppermute | solution.py:21
  22.6 7.7 %collective-permute-done.3 = f32[5,1,128,128]{3,2,1,0:T(8,128)S(1)} collective-permute-done((f32[5,1,128,128]{3,2,1,0:T(8,128)S(1)}, f32[5,1,128,128]{3,2,1,0:T(8,128)S(1)}, u32[]{:S(2)}, u32[]{:S(2)}) %collective-permute-start.3) | collective-permute-done | bytes 327712 | tf_op jit(solution)/shard_map/ppermute | solution.py:24
  38.5 5.5 %collective-permute-done.5 = f32[2,128,128]{2,1,0:T(8,128)S(1)} collective-permute-done((f32[2,128,128]{2,1,0:T(8,128)S(1)}, f32[2,128,128]{2,1,0:T(8,128)S(1)}, u32[]{:S(2)}, u32[]{:S(2)}) %collective-permute-start.5) | collective-permute-done | bytes 131104 | tf_op jit(solution)/shard_map/ppermute | solution.py:24
  52.5 5.5 %collective-permute-done.7 = f32[2,128,128]{2,1,0:T(8,128)S(1)} collective-permute-done((f32[2,128,128]{2,1,0:T(8,128)S(1)}, f32[2,128,128]{2,1,0:T(8,128)S(1)}, u32[]{:S(2)}, u32[]{:S(2)}) %collective-permute-start.7) | collective-permute-done | bytes 131104 | tf_op jit(solution)/shard_map/ppermute | solution.py:24
  59.7 7.9 %collective-permute-done.8 = f32[4,128,128]{2,1,0:T(8,128)S(1)} collective-permute-done((f32[4,128,128]{2,1,0:T(8,128)S(1)}, f32[4,128,128]{2,1,0:T(8,128)S(1)}, u32[]{:S(2)}, u32[]{:S(2)}) %collective-permute-start.8) | collective-permute-done | bytes 262176 | tf_op jit(solution)/shard_map/ppermute | solution.py:32
  74.6 5.5 %collective-permute-done.10 = f32[2,128,128]{2,1,0:T(8,128)S(1)} collective-permute-done((f32[2,128,128]{2,1,0:T(8,128)S(1)}, f32[2,128,128]{2,1,0:T(8,128)S(1)}, u32[]{:S(2)}, u32[]{:S(2)}) %collective-permute-start.10) | collective-permute-done | bytes 131104 | tf_op jit(solution)/shard_map/ppermute | solution.py:24
  81.7 8.0 %collective-permute-done.11 = f32[4,128,128]{2,1,0:T(8,128)S(1)} collective-permute-done((f32[4,128,128]{2,1,0:T(8,128)S(1)}, f32[4,128,128]{2,1,0:T(8,128)S(1)}, u32[]{:S(2)}, u32[]{:S(2)}) %collective-permute-start.11) | collective-permute-done | bytes 262176 | tf_op jit(solution)/shard_map/ppermute | solution.py:32
  96.9 14.6 %collective-permute-done.12 = f32[8,128,128]{2,1,0:T(8,128)} collective-permute-done((f32[8,128,128]{2,1,0:T(8,128)S(1)}, f32[8,128,128]{2,1,0:T(8,128)}, u32[]{:S(2)}, u32[]{:S(2)}) %collective-permute-start.12) | collective-permute-done | bytes 524320 | tf_op jit(solution)/shard_map/ppermute | solution.py:32
  113.1 6.6 %collective-permute-done.13 = f32[8,128,128]{2,1,0:T(8,128)S(1)} collective-permute-done((f32[8,128,128]{2,1,0:T(8,128)S(1)}, f32[8,128,128]{2,1,0:T(8,128)S(1)}, u32[]{:S(2)}, u32[]{:S(2)}) %collective-permute-start.13) | collective-permute-done | bytes 524320 | tf_op jit(solution)/shard_map/ppermute | solution.py:32
  119.7 16.8 %collective-permute-start.18 = (f32[8,128,128]{2,1,0:T(8,128)S(1)}, f32[8,128,128]{2,1,0:T(8,128)S(1)}, u32[]{:S(2)}, u32[]{:S(2)}) collective-permute-start(f32[8,128,128]{2,1,0:T(8,128)S(1)} %constant_dynamic-update-slice_fusion.3), channel_id=1, source_target_pairs={{0,7},{1,0},{2,1},{3,2},{4,3},{5,4},{6,5},{7,6},{8,15},{9,8},{10,9... | collective-permute-start | bytes 1572872 | tf_op jit(solution)/shard_map/ppermute | solution.py:32
  157.8 16.8 %collective-permute-start.19 = (f32[4,128,128]{2,1,0:T(8,128)S(1)}, f32[4,128,128]{2,1,0:T(8,128)S(1)}, u32[]{:S(2)}, u32[]{:S(2)}) collective-permute-start(f32[4,128,128]{2,1,0:T(8,128)S(1)} %add.396), channel_id=1, source_target_pairs={{0,16},{8,24},{16,32},{24,40},{32,48},{40,56},{48,64},{56,72},{64,... | collective-permute-start | bytes 786440 | tf_op jit(solution)/shard_map/ppermute | solution.py:32
  174.6 6.3 %collective-permute-done.19 = f32[4,128,128]{2,1,0:T(8,128)S(1)} collective-permute-done((f32[4,128,128]{2,1,0:T(8,128)S(1)}, f32[4,128,128]{2,1,0:T(8,128)S(1)}, u32[]{:S(2)}, u32[]{:S(2)}) %collective-permute-start.19) | collective-permute-done | bytes 262176 | tf_op jit(solution)/shard_map/ppermute | solution.py:32
  198.7 9.1 %collective-permute-done.23 = f32[4,128,128]{2,1,0:T(8,128)S(1)} collective-permute-done((f32[4,128,128]{2,1,0:T(8,128)S(1)}, f32[4,128,128]{2,1,0:T(8,128)S(1)}, u32[]{:S(2)}, u32[]{:S(2)}) %collective-permute-start.23) | collective-permute-done | bytes 262176 | tf_op jit(solution)/shard_map/ppermute | solution.py:32
  212.5 6.4 %shard_map.38 = f32[4,128,128]{2,1,0:T(8,128)S(1)} custom-call(s32[2]{0:T(128)S(1)} %pad_add_fusion.1.place_ref, f32[8,4,128,128]{3,2,1,0:T(8,128)S(1)} %bitcast_dynamic-update-slice_fusion.32.slots_ref, f32[32,128,128]{2,1,0:T(8,128)S(1)} %get-tuple-element.22.w_ref, f32[32,128,128]{2,1,0:T(8,128)} %get-tuple-element.21.s_ref), custom_call_target="tpu_custom_call" | custom-call | flops 25165824 | bytes 6291456 | tf_op jit(solution)/shard_map/pallas_call | solution.py:103
  222.0 9.5 %collective-permute-done.27 = f32[4,128,128]{2,1,0:T(8,128)S(1)} collective-permute-done((f32[4,128,128]{2,1,0:T(8,128)S(1)}, f32[4,128,128]{2,1,0:T(8,128)S(1)}, u32[]{:S(2)}, u32[]{:S(2)}) %collective-permute-start.27) | collective-permute-done | bytes 262176 | tf_op jit(solution)/shard_map/ppermute | solution.py:32
  250.1 6.0 %collective-permute-done.31 = f32[4,128,128]{2,1,0:T(8,128)S(1)} collective-permute-done((f32[4,128,128]{2,1,0:T(8,128)S(1)}, f32[4,128,128]{2,1,0:T(8,128)S(1)}, u32[]{:S(2)}, u32[]{:S(2)}) %collective-permute-start.31) | collective-permute-done | bytes 262176 | tf_op jit(solution)/shard_map/ppermute | solution.py:32
  256.7 7.4 %collective-permute-done.33 = f32[4,128,128]{2,1,0:T(8,128)S(1)} collective-permute-done((f32[4,128,128]{2,1,0:T(8,128)S(1)}, f32[4,128,128]{2,1,0:T(8,128)S(1)}, u32[]{:S(2)}, u32[]{:S(2)}) %collective-permute-start.33) | collective-permute-done | bytes 262176 | tf_op jit(solution)/shard_map/ppermute | solution.py:32
  264.5 10.7 %shard_map.39 = f32[4,128,128]{2,1,0:T(8,128)S(1)} custom-call(s32[2]{0:T(128)S(1)} %pad_add_fusion.2.place_ref, f32[8,4,128,128]{3,2,1,0:T(8,128)S(1)} %bitcast_dynamic-update-slice_fusion.24.slots_ref, f32[32,128,128]{2,1,0:T(8,128)S(1)} %get-tuple-element.22.w_ref, f32[32,128,128]{2,1,0:T(8,128)} %get-tuple-element.21.s_ref), custom_call_target="tpu_custom_call" | custom-call | flops 50331648 | bytes 6291456 | tf_op jit(solution)/shard_map/pallas_call | solution.py:103
  276.6 11.9 %collective-permute-done.35 = f32[4,128,128]{2,1,0:T(8,128)S(1)} collective-permute-done((f32[4,128,128]{2,1,0:T(8,128)S(1)}, f32[4,128,128]{2,1,0:T(8,128)S(1)}, u32[]{:S(2)}, u32[]{:S(2)}) %collective-permute-start.35) | collective-permute-done | bytes 262176 | tf_op jit(solution)/shard_map/ppermute | solution.py:32
  304.0 5.5 %collective-permute-done.38 = f32[4,128,128]{2,1,0:T(8,128)S(1)} collective-permute-done((f32[4,128,128]{2,1,0:T(8,128)S(1)}, f32[4,128,128]{2,1,0:T(8,128)S(1)}, u32[]{:S(2)}, u32[]{:S(2)}) %collective-permute-start.38) | collective-permute-done | bytes 262176 | tf_op jit(solution)/shard_map/ppermute | solution.py:32
  309.5 5.6 %collective-permute-done.39 = f32[4,128,128]{2,1,0:T(8,128)S(1)} collective-permute-done((f32[4,128,128]{2,1,0:T(8,128)S(1)}, f32[4,128,128]{2,1,0:T(8,128)S(1)}, u32[]{:S(2)}, u32[]{:S(2)}) %collective-permute-start.39) | collective-permute-done | bytes 262176 | tf_op jit(solution)/shard_map/ppermute | solution.py:32
  315.2 8.0 %collective-permute-done.41 = f32[4,128,128]{2,1,0:T(8,128)S(1)} collective-permute-done((f32[4,128,128]{2,1,0:T(8,128)S(1)}, f32[4,128,128]{2,1,0:T(8,128)S(1)}, u32[]{:S(2)}, u32[]{:S(2)}) %collective-permute-start.41) | collective-permute-done | bytes 262176 | tf_op jit(solution)/shard_map/ppermute | solution.py:32
  324.8 19.6 %shard_map.40 = f32[4,128,128]{2,1,0:T(8,128)S(1)} custom-call(s32[2]{0:T(128)S(1)} %pad_add_fusion.3.place_ref, f32[8,4,128,128]{3,2,1,0:T(8,128)S(1)} %bitcast_dynamic-update-slice_fusion.16.slots_ref, f32[32,128,128]{2,1,0:T(8,128)S(1)} %get-tuple-element.22.w_ref, f32[32,128,128]{2,1,0:T(8,128)} %get-tuple-element.21.s_ref), custom_call_target="tpu_custom_call" | custom-call | flops 100663296 | bytes 6291456 | tf_op jit(solution)/shard_map/pallas_call | solution.py:103
  344.4 5.4 %collective-permute-start.43 = (f32[4,128,128]{2,1,0:T(8,128)S(1)}, f32[4,128,128]{2,1,0:T(8,128)S(1)}, u32[]{:S(2)}, u32[]{:S(2)}) collective-permute-start(f32[4,128,128]{2,1,0:T(8,128)S(1)} %add.399), channel_id=1, source_target_pairs={{0,128},{8,136},{16,144},{24,152},{32,160},{40,168},{48,176},{56,1... | collective-permute-start | bytes 786440 | tf_op jit(solution)/shard_map/ppermute | solution.py:32
  349.9 11.4 %collective-permute-done.43 = f32[4,128,128]{2,1,0:T(8,128)S(1)} collective-permute-done((f32[4,128,128]{2,1,0:T(8,128)S(1)}, f32[4,128,128]{2,1,0:T(8,128)S(1)}, u32[]{:S(2)}, u32[]{:S(2)}) %collective-permute-start.43) | collective-permute-done | bytes 262176 | tf_op jit(solution)/shard_map/ppermute | solution.py:32
  361.4 5.8 %collective-permute-start.46 = (f32[4,128,128]{2,1,0:T(8,128)S(1)}, f32[4,128,128]{2,1,0:T(8,128)S(1)}, u32[]{:S(2)}, u32[]{:S(2)}) collective-permute-start(f32[4,128,128]{2,1,0:T(8,128)S(1)} %collective-permute-done.43), channel_id=1, source_target_pairs={{0,3},{1,4},{2,5},{3,6},{4,7},{5,0},{6,1},{7,2},{8,11},{9,12},{10,... | collective-permute-start | bytes 786440 | tf_op jit(solution)/shard_map/ppermute | solution.py:32
  379.4 8.7 %collective-permute-done.47 = f32[4,128,128]{2,1,0:T(8,128)S(1)} collective-permute-done((f32[4,128,128]{2,1,0:T(8,128)S(1)}, f32[4,128,128]{2,1,0:T(8,128)S(1)}, u32[]{:S(2)}, u32[]{:S(2)}) %collective-permute-start.47) | collective-permute-done | bytes 262176 | tf_op jit(solution)/shard_map/ppermute | solution.py:32
  388.2 9.2 %collective-permute-done.49 = f32[4,128,128]{2,1,0:T(8,128)S(1)} collective-permute-done((f32[4,128,128]{2,1,0:T(8,128)S(1)}, f32[4,128,128]{2,1,0:T(8,128)S(1)}, u32[]{:S(2)}, u32[]{:S(2)}) %collective-permute-start.49) | collective-permute-done | bytes 262176 | tf_op jit(solution)/shard_map/ppermute | solution.py:32
  398.8 37.5 %shard_map.41 = f32[4,128,128]{2,1,0:T(8,128)S(1)} custom-call(s32[2]{0:T(128)S(1)} %pad_add_fusion.4.place_ref, f32[8,4,128,128]{3,2,1,0:T(8,128)S(1)} %bitcast_dynamic-update-slice_fusion.8.slots_ref, f32[32,128,128]{2,1,0:T(8,128)S(1)} %get-tuple-element.22.w_ref, f32[32,128,128]{2,1,0:T(8,128)} %get-tuple-element.21.s_ref), custom_call_target="tpu_custom_call" | custom-call | flops 201326592 | bytes 6291456 | tf_op jit(solution)/shard_map/pallas_call | solution.py:103
  443.2 5.5 %collective-permute-done.52 = f32[2,128,128]{2,1,0:T(8,128)S(1)} collective-permute-done((f32[2,128,128]{2,1,0:T(8,128)S(1)}, f32[2,128,128]{2,1,0:T(8,128)S(1)}, u32[]{:S(2)}, u32[]{:S(2)}) %collective-permute-start.52) | collective-permute-done | bytes 131104 | tf_op jit(solution)/shard_map/ppermute | solution.py:24
  458.2 5.5 %collective-permute-done.54 = f32[2,128,128]{2,1,0:T(8,128)S(1)} collective-permute-done((f32[2,128,128]{2,1,0:T(8,128)S(1)}, f32[2,128,128]{2,1,0:T(8,128)S(1)}, u32[]{:S(2)}, u32[]{:S(2)}) %collective-permute-start.54) | collective-permute-done | bytes 131104 | tf_op jit(solution)/shard_map/ppermute | solution.py:24
  472.2 5.5 %collective-permute-done.56 = f32[2,128,128]{2,1,0:T(8,128)S(1)} collective-permute-done((f32[2,128,128]{2,1,0:T(8,128)S(1)}, f32[2,128,128]{2,1,0:T(8,128)S(1)}, u32[]{:S(2)}, u32[]{:S(2)}) %collective-permute-start.56) | collective-permute-done | bytes 131104 | tf_op jit(solution)/shard_map/ppermute | solution.py:24
  (241 shorter events, 175.9 us)
Async XLA Ops:
  1.0 17.1 %collective-permute-start = (f32[2,128,128]{2,1,0:T(8,128)S(1)}, f32[2,128,128]{2,1,0:T(8,128)S(1)}, u32[]{:S(2)}, u32[]{:S(2)}) collective-permute-start(f32[2,128,128]{2,1,0:T(8,128)S(1)} %get-tuple-element.139), channel_id=1, source_target_pairs={{0,1},{1,2},{2,3},{3,4},{4,5},{5,6},{6,7},{8,9},{9,10},{10,11},{11... | collective-permute-start | bytes 393224 | tf_op jit(solution)/shard_map/ppermute | solution.py:21
  89.8 21.8 %collective-permute-start.12 = (f32[8,128,128]{2,1,0:T(8,128)S(1)}, f32[8,128,128]{2,1,0:T(8,128)}, u32[]{:S(2)}, u32[]{:S(2)}) collective-permute-start(f32[8,128,128]{2,1,0:T(8,128)S(1)} %constant_dynamic-update-slice_fusion.3), channel_id=1, source_target_pairs={{0,1},{1,2},{2,3},{3,4},{4,5},{5,6},{6,7},{7,0},{8,9},{9,10},{10,1... | collective-permute-start | bytes 1572872 | tf_op jit(solution)/shard_map/ppermute | solution.py:32
  89.9 29.8 %collective-permute-start.13 = (f32[8,128,128]{2,1,0:T(8,128)S(1)}, f32[8,128,128]{2,1,0:T(8,128)S(1)}, u32[]{:S(2)}, u32[]{:S(2)}) collective-permute-start(f32[8,128,128]{2,1,0:T(8,128)S(1)} %constant_dynamic-update-slice_fusion.3), channel_id=1, source_target_pairs={{0,2},{1,3},{2,4},{3,5},{4,6},{5,7},{6,0},{7,1},{8,10},{9,11},{10,... | collective-permute-start | bytes 1572872 | tf_op jit(solution)/shard_map/ppermute | solution.py:32
  90.2 46.3 %collective-permute-start.14 = (f32[8,128,128]{2,1,0:T(8,128)S(1)}, f32[8,128,128]{2,1,0:T(8,128)S(1)}, u32[]{:S(2)}, u32[]{:S(2)}) collective-permute-start(f32[8,128,128]{2,1,0:T(8,128)S(1)} %constant_dynamic-update-slice_fusion.3), channel_id=1, source_target_pairs={{0,3},{1,4},{2,5},{3,6},{4,7},{5,0},{6,1},{7,2},{8,11},{9,12},{10,... | collective-permute-start | bytes 1572872 | tf_op jit(solution)/shard_map/ppermute | solution.py:32
  92.4 45.1 %collective-permute-start.15 = (f32[8,128,128]{2,1,0:T(8,128)S(1)}, f32[8,128,128]{2,1,0:T(8,128)S(1)}, u32[]{:S(2)}, u32[]{:S(2)}) collective-permute-start(f32[8,128,128]{2,1,0:T(8,128)S(1)} %constant_dynamic-update-slice_fusion.3), channel_id=1, source_target_pairs={{0,4},{1,5},{2,6},{3,7},{4,0},{5,1},{6,2},{7,3},{8,12},{9,13},{10,... | collective-permute-start | bytes 1572872 | tf_op jit(solution)/shard_map/ppermute | solution.py:32
  95.3 42.2 %collective-permute-start.16 = (f32[8,128,128]{2,1,0:T(8,128)S(1)}, f32[8,128,128]{2,1,0:T(8,128)S(1)}, u32[]{:S(2)}, u32[]{:S(2)}) collective-permute-start(f32[8,128,128]{2,1,0:T(8,128)S(1)} %constant_dynamic-update-slice_fusion.3), channel_id=1, source_target_pairs={{0,5},{1,6},{2,7},{3,0},{4,1},{5,2},{6,3},{7,4},{8,13},{9,14},{10,... | collective-permute-start | bytes 1572872 | tf_op jit(solution)/shard_map/ppermute | solution.py:32
  111.6 31.1 %collective-permute-start.17 = (f32[8,128,128]{2,1,0:T(8,128)S(1)}, f32[8,128,128]{2,1,0:T(8,128)S(1)}, u32[]{:S(2)}, u32[]{:S(2)}) collective-permute-start(f32[8,128,128]{2,1,0:T(8,128)S(1)} %constant_dynamic-update-slice_fusion.3), channel_id=1, source_target_pairs={{0,6},{1,7},{2,0},{3,1},{4,2},{5,3},{6,4},{7,5},{8,14},{9,15},{10,... | collective-permute-start | bytes 1572872 | tf_op jit(solution)/shard_map/ppermute | solution.py:32
  119.7 25.3 %collective-permute-start.18 = (f32[8,128,128]{2,1,0:T(8,128)S(1)}, f32[8,128,128]{2,1,0:T(8,128)S(1)}, u32[]{:S(2)}, u32[]{:S(2)}) collective-permute-start(f32[8,128,128]{2,1,0:T(8,128)S(1)} %constant_dynamic-update-slice_fusion.3), channel_id=1, source_target_pairs={{0,7},{1,0},{2,1},{3,2},{4,3},{5,4},{6,5},{7,6},{8,15},{9,8},{10,9... | collective-permute-start | bytes 1572872 | tf_op jit(solution)/shard_map/ppermute | solution.py:32
  157.8 23.1 %collective-permute-start.19 = (f32[4,128,128]{2,1,0:T(8,128)S(1)}, f32[4,128,128]{2,1,0:T(8,128)S(1)}, u32[]{:S(2)}, u32[]{:S(2)}) collective-permute-start(f32[4,128,128]{2,1,0:T(8,128)S(1)} %add.396), channel_id=1, source_target_pairs={{0,16},{8,24},{16,32},{24,40},{32,48},{40,56},{48,64},{56,72},{64,... | collective-permute-start | bytes 786440 | tf_op jit(solution)/shard_map/ppermute | solution.py:32
  181.0 17.7 %collective-permute-start.22 = (f32[4,128,128]{2,1,0:T(8,128)S(1)}, f32[4,128,128]{2,1,0:T(8,128)S(1)}, u32[]{:S(2)}, u32[]{:S(2)}) collective-permute-start(f32[4,128,128]{2,1,0:T(8,128)S(1)} %collective-permute-done.19), channel_id=1, source_target_pairs={{0,3},{1,4},{2,5},{3,6},{4,7},{5,0},{6,1},{7,2},{8,11},{9,12},{10,... | collective-permute-start | bytes 786440 | tf_op jit(solution)/shard_map/ppermute | solution.py:32
  185.5 22.4 %collective-permute-start.23 = (f32[4,128,128]{2,1,0:T(8,128)S(1)}, f32[4,128,128]{2,1,0:T(8,128)S(1)}, u32[]{:S(2)}, u32[]{:S(2)}) collective-permute-start(f32[4,128,128]{2,1,0:T(8,128)S(1)} %collective-permute-done.19), channel_id=1, source_target_pairs={{0,4},{1,5},{2,6},{3,7},{4,0},{5,1},{6,2},{7,3},{8,12},{9,13},{10,... | collective-permute-start | bytes 786440 | tf_op jit(solution)/shard_map/ppermute | solution.py:32
  186.1 21.8 %collective-permute-start.24 = (f32[4,128,128]{2,1,0:T(8,128)S(1)}, f32[4,128,128]{2,1,0:T(8,128)S(1)}, u32[]{:S(2)}, u32[]{:S(2)}) collective-permute-start(f32[4,128,128]{2,1,0:T(8,128)S(1)} %collective-permute-done.19), channel_id=1, source_target_pairs={{0,5},{1,6},{2,7},{3,0},{4,1},{5,2},{6,3},{7,4},{8,13},{9,14},{10,... | collective-permute-start | bytes 786440 | tf_op jit(solution)/shard_map/ppermute | solution.py:32
  190.4 22.0 %collective-permute-start.25 = (f32[4,128,128]{2,1,0:T(8,128)S(1)}, f32[4,128,128]{2,1,0:T(8,128)S(1)}, u32[]{:S(2)}, u32[]{:S(2)}) collective-permute-start(f32[4,128,128]{2,1,0:T(8,128)S(1)} %collective-permute-done.19), channel_id=1, source_target_pairs={{0,6},{1,7},{2,0},{3,1},{4,2},{5,3},{6,4},{7,5},{8,14},{9,15},{10,... | collective-permute-start | bytes 786440 | tf_op jit(solution)/shard_map/ppermute | solution.py:32
  193.7 18.8 %collective-permute-start.26 = (f32[4,128,128]{2,1,0:T(8,128)S(1)}, f32[4,128,128]{2,1,0:T(8,128)S(1)}, u32[]{:S(2)}, u32[]{:S(2)}) collective-permute-start(f32[4,128,128]{2,1,0:T(8,128)S(1)} %collective-permute-done.19), channel_id=1, source_target_pairs={{0,7},{1,0},{2,1},{3,2},{4,3},{5,4},{6,5},{7,6},{8,15},{9,8},{10,9... | collective-permute-start | bytes 786440 | tf_op jit(solution)/shard_map/ppermute | solution.py:32
  232.8 17.2 %collective-permute-start.30 = (f32[4,128,128]{2,1,0:T(8,128)S(1)}, f32[4,128,128]{2,1,0:T(8,128)S(1)}, u32[]{:S(2)}, u32[]{:S(2)}) collective-permute-start(f32[4,128,128]{2,1,0:T(8,128)S(1)} %collective-permute-done.27), channel_id=1, source_target_pairs={{0,3},{1,4},{2,5},{3,6},{4,7},{5,0},{6,1},{7,2},{8,11},{9,12},{10,... | collective-permute-start | bytes 786440 | tf_op jit(solution)/shard_map/ppermute | solution.py:32
  236.2 19.8 %collective-permute-start.31 = (f32[4,128,128]{2,1,0:T(8,128)S(1)}, f32[4,128,128]{2,1,0:T(8,128)S(1)}, u32[]{:S(2)}, u32[]{:S(2)}) collective-permute-start(f32[4,128,128]{2,1,0:T(8,128)S(1)} %collective-permute-done.27), channel_id=1, source_target_pairs={{0,4},{1,5},{2,6},{3,7},{4,0},{5,1},{6,2},{7,3},{8,12},{9,13},{10,... | collective-permute-start | bytes 786440 | tf_op jit(solution)/shard_map/ppermute | solution.py:32
  239.3 17.3 %collective-permute-start.32 = (f32[4,128,128]{2,1,0:T(8,128)S(1)}, f32[4,128,128]{2,1,0:T(8,128)S(1)}, u32[]{:S(2)}, u32[]{:S(2)}) collective-permute-start(f32[4,128,128]{2,1,0:T(8,128)S(1)} %collective-permute-done.27), channel_id=1, source_target_pairs={{0,5},{1,6},{2,7},{3,0},{4,1},{5,2},{6,3},{7,4},{8,13},{9,14},{10,... | collective-permute-start | bytes 786440 | tf_op jit(solution)/shard_map/ppermute | solution.py:32
  244.0 20.1 %collective-permute-start.33 = (f32[4,128,128]{2,1,0:T(8,128)S(1)}, f32[4,128,128]{2,1,0:T(8,128)S(1)}, u32[]{:S(2)}, u32[]{:S(2)}) collective-permute-start(f32[4,128,128]{2,1,0:T(8,128)S(1)} %collective-permute-done.27), channel_id=1, source_target_pairs={{0,6},{1,7},{2,0},{3,1},{4,2},{5,3},{6,4},{7,5},{8,14},{9,15},{10,... | collective-permute-start | bytes 786440 | tf_op jit(solution)/shard_map/ppermute | solution.py:32
  245.5 19.0 %collective-permute-start.34 = (f32[4,128,128]{2,1,0:T(8,128)S(1)}, f32[4,128,128]{2,1,0:T(8,128)S(1)}, u32[]{:S(2)}, u32[]{:S(2)}) collective-permute-start(f32[4,128,128]{2,1,0:T(8,128)S(1)} %collective-permute-done.27), channel_id=1, source_target_pairs={{0,7},{1,0},{2,1},{3,2},{4,3},{5,4},{6,5},{7,6},{8,15},{9,8},{10,9... | collective-permute-start | bytes 786440 | tf_op jit(solution)/shard_map/ppermute | solution.py:32
  288.7 15.1 %collective-permute-start.37 = (f32[4,128,128]{2,1,0:T(8,128)S(1)}, f32[4,128,128]{2,1,0:T(8,128)S(1)}, u32[]{:S(2)}, u32[]{:S(2)}) collective-permute-start(f32[4,128,128]{2,1,0:T(8,128)S(1)} %collective-permute-done.35), channel_id=1, source_target_pairs={{0,2},{1,3},{2,4},{3,5},{4,6},{5,7},{6,0},{7,1},{8,10},{9,11},{10,... | collective-permute-start | bytes 786440 | tf_op jit(solution)/shard_map/ppermute | solution.py:32
  292.8 16.7 %collective-permute-start.38 = (f32[4,128,128]{2,1,0:T(8,128)S(1)}, f32[4,128,128]{2,1,0:T(8,128)S(1)}, u32[]{:S(2)}, u32[]{:S(2)}) collective-permute-start(f32[4,128,128]{2,1,0:T(8,128)S(1)} %collective-permute-done.35), channel_id=1, source_target_pairs={{0,3},{1,4},{2,5},{3,6},{4,7},{5,0},{6,1},{7,2},{8,11},{9,12},{10,... | collective-permute-start | bytes 786440 | tf_op jit(solution)/shard_map/ppermute | solution.py:32
  292.9 22.3 %collective-permute-start.39 = (f32[4,128,128]{2,1,0:T(8,128)S(1)}, f32[4,128,128]{2,1,0:T(8,128)S(1)}, u32[]{:S(2)}, u32[]{:S(2)}) collective-permute-start(f32[4,128,128]{2,1,0:T(8,128)S(1)} %collective-permute-done.35), channel_id=1, source_target_pairs={{0,4},{1,5},{2,6},{3,7},{4,0},{5,1},{6,2},{7,3},{8,12},{9,13},{10,... | collective-permute-start | bytes 786440 | tf_op jit(solution)/shard_map/ppermute | solution.py:32
  295.3 19.9 %collective-permute-start.40 = (f32[4,128,128]{2,1,0:T(8,128)S(1)}, f32[4,128,128]{2,1,0:T(8,128)S(1)}, u32[]{:S(2)}, u32[]{:S(2)}) collective-permute-start(f32[4,128,128]{2,1,0:T(8,128)S(1)} %collective-permute-done.35), channel_id=1, source_target_pairs={{0,5},{1,6},{2,7},{3,0},{4,1},{5,2},{6,3},{7,4},{8,13},{9,14},{10,... | collective-permute-start | bytes 786440 | tf_op jit(solution)/shard_map/ppermute | solution.py:32
  302.1 21.1 %collective-permute-start.41 = (f32[4,128,128]{2,1,0:T(8,128)S(1)}, f32[4,128,128]{2,1,0:T(8,128)S(1)}, u32[]{:S(2)}, u32[]{:S(2)}) collective-permute-start(f32[4,128,128]{2,1,0:T(8,128)S(1)} %collective-permute-done.35), channel_id=1, source_target_pairs={{0,6},{1,7},{2,0},{3,1},{4,2},{5,3},{6,4},{7,5},{8,14},{9,15},{10,... | collective-permute-start | bytes 786440 | tf_op jit(solution)/shard_map/ppermute | solution.py:32
  303.8 20.9 %collective-permute-start.42 = (f32[4,128,128]{2,1,0:T(8,128)S(1)}, f32[4,128,128]{2,1,0:T(8,128)S(1)}, u32[]{:S(2)}, u32[]{:S(2)}) collective-permute-start(f32[4,128,128]{2,1,0:T(8,128)S(1)} %collective-permute-done.35), channel_id=1, source_target_pairs={{0,7},{1,0},{2,1},{3,2},{4,3},{5,4},{6,5},{7,6},{8,15},{9,8},{10,9... | collective-permute-start | bytes 786440 | tf_op jit(solution)/shard_map/ppermute | solution.py:32
  344.4 16.8 %collective-permute-start.43 = (f32[4,128,128]{2,1,0:T(8,128)S(1)}, f32[4,128,128]{2,1,0:T(8,128)S(1)}, u32[]{:S(2)}, u32[]{:S(2)}) collective-permute-start(f32[4,128,128]{2,1,0:T(8,128)S(1)} %add.399), channel_id=1, source_target_pairs={{0,128},{8,136},{16,144},{24,152},{32,160},{40,168},{48,176},{56,1... | collective-permute-start | bytes 786440 | tf_op jit(solution)/shard_map/ppermute | solution.py:32
  361.4 16.2 %collective-permute-start.45 = (f32[4,128,128]{2,1,0:T(8,128)S(1)}, f32[4,128,128]{2,1,0:T(8,128)S(1)}, u32[]{:S(2)}, u32[]{:S(2)}) collective-permute-start(f32[4,128,128]{2,1,0:T(8,128)S(1)} %collective-permute-done.43), channel_id=1, source_target_pairs={{0,2},{1,3},{2,4},{3,5},{4,6},{5,7},{6,0},{7,1},{8,10},{9,11},{10,... | collective-permute-start | bytes 786440 | tf_op jit(solution)/shard_map/ppermute | solution.py:32
  361.4 17.9 %collective-permute-start.46 = (f32[4,128,128]{2,1,0:T(8,128)S(1)}, f32[4,128,128]{2,1,0:T(8,128)S(1)}, u32[]{:S(2)}, u32[]{:S(2)}) collective-permute-start(f32[4,128,128]{2,1,0:T(8,128)S(1)} %collective-permute-done.43), channel_id=1, source_target_pairs={{0,3},{1,4},{2,5},{3,6},{4,7},{5,0},{6,1},{7,2},{8,11},{9,12},{10,... | collective-permute-start | bytes 786440 | tf_op jit(solution)/shard_map/ppermute | solution.py:32
  367.3 20.8 %collective-permute-start.47 = (f32[4,128,128]{2,1,0:T(8,128)S(1)}, f32[4,128,128]{2,1,0:T(8,128)S(1)}, u32[]{:S(2)}, u32[]{:S(2)}) collective-permute-start(f32[4,128,128]{2,1,0:T(8,128)S(1)} %collective-permute-done.43), channel_id=1, source_target_pairs={{0,4},{1,5},{2,6},{3,7},{4,0},{5,1},{6,2},{7,3},{8,12},{9,13},{10,... | collective-permute-start | bytes 786440 | tf_op jit(solution)/shard_map/ppermute | solution.py:32
  368.8 19.4 %collective-permute-start.48 = (f32[4,128,128]{2,1,0:T(8,128)S(1)}, f32[4,128,128]{2,1,0:T(8,128)S(1)}, u32[]{:S(2)}, u32[]{:S(2)}) collective-permute-start(f32[4,128,128]{2,1,0:T(8,128)S(1)} %collective-permute-done.43), channel_id=1, source_target_pairs={{0,5},{1,6},{2,7},{3,0},{4,1},{5,2},{6,3},{7,4},{8,13},{9,14},{10,... | collective-permute-start | bytes 786440 | tf_op jit(solution)/shard_map/ppermute | solution.py:32
  374.4 23.0 %collective-permute-start.49 = (f32[4,128,128]{2,1,0:T(8,128)S(1)}, f32[4,128,128]{2,1,0:T(8,128)S(1)}, u32[]{:S(2)}, u32[]{:S(2)}) collective-permute-start(f32[4,128,128]{2,1,0:T(8,128)S(1)} %collective-permute-done.43), channel_id=1, source_target_pairs={{0,6},{1,7},{2,0},{3,1},{4,2},{5,3},{6,4},{7,5},{8,14},{9,15},{10,... | collective-permute-start | bytes 786440 | tf_op jit(solution)/shard_map/ppermute | solution.py:32
  377.5 21.2 %collective-permute-start.50 = (f32[4,128,128]{2,1,0:T(8,128)S(1)}, f32[4,128,128]{2,1,0:T(8,128)S(1)}, u32[]{:S(2)}, u32[]{:S(2)}) collective-permute-start(f32[4,128,128]{2,1,0:T(8,128)S(1)} %collective-permute-done.43), channel_id=1, source_target_pairs={{0,7},{1,0},{2,1},{3,2},{4,3},{5,4},{6,5},{7,6},{8,15},{9,8},{10,9... | collective-permute-start | bytes 786440 | tf_op jit(solution)/shard_map/ppermute | solution.py:32
  (30 other events, 355.6 us)
